TPU v7x, 256 devices: a whole 4x4x8 slice. The times are simulated.
256 devices in a mesh: seq: 32 (over y, z), ch: 8 (over x, core).
Axes of the slice: x: 4, y: 4, z: 8, core: 2. Of those that a mesh axis runs over, the one named last changes fastest.
Arguments:
- hidden_in: bfloat16 [65536, 2048], P('seq', 'ch'), may hold values from -6 to 6
- grad_out: bfloat16 [65536, 2048], P('seq', 'ch'), may hold values from -6 to 6
- norm_gain: bfloat16 [2048], P('ch'), may hold values from 0.099609375 to 1.8984375
- skip_weight: float32 [2048], P('ch'), may hold values from -4 to 4
- filter_coef: bfloat16 [64, 2, 2048], P(None, None, 'ch'), may hold values from -0.75 to 0.75
- run_lengths: int32 [64], replicated, may hold values from 1 to 4096, 65536 in all
Outputs:
- hidden_grad: bfloat16 [65536, 2048], P('seq', 'ch')
- filter_grad: float32 [64, 2, 2048], P('seq', None, 'ch')
Inputs may be any that keep to these rules, and one draw needn't show every extreme that they name: `run_lengths`: runs lie end to end from token 0, documents at even positions and padding at odd ones; they sum to 65536, and the longest has exactly 4096 tokens.
All inputs are finite; a program needn't handle non-finite values.
Results may differ from a plain program's by a relative error of at most 0.0095.
Values may be sent and summed in bfloat16 or wider, within the bound.
No kernel may reach another device: no remote copies, remote signals or barrier semaphores. Data moves between devices by JAX's collectives and lax.ppermute only.
A program may use at most 64 MiB of HBM per device.

v0:
```python
import math

import jax
import jax.numpy as jnp
from jax import lax
from jax.sharding import PartitionSpec as P

D = 2048
BLOCK = 512
FEAT = 64


epsilon = 1e-06


def from_everyone(value, axis):
    copies = jnp.broadcast_to(value, (lax.axis_size(axis), *value.shape))
    return lax.all_to_all(copies, axis, split_axis=0, concat_axis=0, tiled=True)


def taken_together(value, axis):
    count = lax.axis_size(axis)
    step = 1
    while step < count:
        pairs = [(i, i ^ step) for i in range(count)]
        value = value + lax.ppermute(value, axis, pairs)
        step *= 2
    return value


def twin_table(count, sign):
    low = 64 if count % 64 == 0 else count
    indices = jnp.arange(count, dtype=jnp.int32)
    low_ids = jnp.arange(low, dtype=jnp.int32)
    high_ids = jnp.arange(count // low, dtype=jnp.int32) * low
    low_ang = 2.0 * math.pi / count * (indices[:, None] * low_ids[None, :] % count).astype(jnp.float32)
    high_ang = 2.0 * math.pi / count * (indices[:, None] * high_ids[None, :] % count).astype(jnp.float32)
    low_cos, low_sin = jnp.cos(low_ang)[:, None, :], jnp.sin(low_ang)[:, None, :]
    high_cos, high_sin = jnp.cos(high_ang)[:, :, None], jnp.sin(high_ang)[:, :, None]
    cosine = (low_cos * high_cos - low_sin * high_sin).reshape(count, count)
    sine = (low_sin * high_cos + low_cos * high_sin).reshape(count, count)
    factor = 1.0 / math.sqrt(count)
    return (cosine * factor, sign * sine * factor)


def block_matrix(count, sign):
    cosine, sine_part = twin_table(count, sign)
    half = jnp.arange(2, dtype=jnp.int32)
    same = (half[:, None, None, None] == half[None, None, :, None])
    upper = half[:, None, None, None] == 0
    sine_signed = jnp.where(upper, sine_part[None, :, None, :], -sine_part[None, :, None, :])
    whole = jnp.where(same, cosine[None, :, None, :], sine_signed)
    return whole.reshape(2 * count, 2 * count)


def twist_leading(parts, freq_index, pos_index, seq_total, sign):
    product = (freq_index[:, None] * pos_index[None, :]).astype(jnp.float32)
    angles = 2.0 * math.pi / seq_total * product
    cosine = jnp.cos(angles)[None, :, :]
    sine_part = (sign * jnp.sin(angles))[None, :, :]
    real_part = parts[:, :, 0] * cosine - parts[:, :, 1] * sine_part
    imag_part = parts[:, :, 0] * sine_part + parts[:, :, 1] * cosine
    return jnp.stack([real_part, imag_part], axis=2)


def features(freq_index, seq_total):
    orders = 2 * jnp.arange(FEAT, dtype=jnp.int32) + 1
    product = freq_index[..., None] * orders % seq_total
    return jnp.cos(2.0 * math.pi / seq_total * product.astype(jnp.float32))


def feature_factors(inner, nblocks, seq_total):
    orders = 2 * jnp.arange(FEAT, dtype=jnp.int32) + 1
    inner_ids = jnp.arange(inner, dtype=jnp.int32)
    block_ids = jnp.arange(nblocks, dtype=jnp.int32)
    inner_prod = (inner_ids[:, None] * orders[None, :]) % inner
    block_prod = (block_ids[:, None] * orders[None, :]) % seq_total
    inner_ang = 2.0 * math.pi / inner * inner_prod.astype(jnp.float32)
    block_ang = 2.0 * math.pi / seq_total * block_prod.astype(jnp.float32)
    inner_tab = jnp.concatenate([jnp.cos(inner_ang), jnp.sin(inner_ang)], axis=1)
    return inner_tab, jnp.cos(block_ang), jnp.sin(block_ang)


def per_device(hidden_in, grad_out, norm_gain, skip_weight, filter_coef, run_lengths):
    local_tokens = hidden_in.shape[0]
    local_width = hidden_in.shape[1]
    seq_parts = lax.axis_size("seq")
    seq_rank = lax.axis_index("seq")
    seq_total = local_tokens * seq_parts
    nblocks = seq_total // BLOCK
    upcast = hidden_in.astype(jnp.float32)
    square_sums = taken_together(jnp.sum(upcast * upcast, axis=1), "ch")
    inverse_rms = lax.rsqrt(square_sums / D + epsilon)
    gain = norm_gain.astype(jnp.float32)
    normed = (upcast * inverse_rms[:, None] * gain[None, :]).astype(jnp.bfloat16)
    run_ends = jnp.cumsum(run_lengths)
    positions = seq_rank * local_tokens + jnp.arange(local_tokens, dtype=jnp.int32)
    run_index = jnp.sum((run_ends[None, :] <= positions[:, None]).astype(jnp.int32), axis=1)
    keep = run_index % 2 == 0
    gated = jnp.where(keep[:, None], grad_out, jnp.zeros_like(grad_out))
    forward_first = jnp.stack(twin_table(nblocks, -1.0), axis=2).astype(jnp.bfloat16)
    forward_second = block_matrix(BLOCK, -1.0).astype(jnp.bfloat16)
    back_first = block_matrix(BLOCK, 1.0).astype(jnp.bfloat16)
    cosine, sine_part = twin_table(nblocks, 1.0)
    back_second = jnp.stack([cosine, -sine_part], axis=1).astype(jnp.bfloat16)
    block_ids = jnp.arange(nblocks, dtype=jnp.int32)
    all_inner = jnp.arange(BLOCK, dtype=jnp.int32)
    width_share = local_width // seq_parts
    gated, inverse_rms = lax.optimization_barrier((gated, inverse_rms))
    gated_moved = lax.all_to_all(gated.T, "seq", split_axis=0, concat_axis=1, tiled=True)
    gated_moved, normed = lax.optimization_barrier((gated_moved, normed))
    normed_moved = lax.all_to_all(normed.T, "seq", split_axis=0, concat_axis=1, tiled=True)
    moved = (normed_moved, gated_moved)
    coef_part = lax.dynamic_slice_in_dim(filter_coef, seq_rank * width_share, width_share, 2)

    def local_freq(field):
        blocks = field.reshape(width_share, nblocks, BLOCK)
        parts = jnp.einsum(
            "cnm,nkr->ckrm", blocks, forward_first, preferred_element_type=jnp.float32
        )
        turned = twist_leading(parts, block_ids, all_inner, seq_total, -1.0).astype(jnp.bfloat16)
        flat = turned.reshape(width_share, nblocks, 2 * BLOCK)
        spectrum = jnp.einsum(
            "ckm,mj->ckj", flat, forward_second, preferred_element_type=jnp.float32
        )
        return spectrum.reshape(width_share, nblocks, 2, BLOCK)

    spec_gated = local_freq(moved[1])
    inner_tab, block_cos, block_sin = feature_factors(BLOCK, nblocks, seq_total)
    coef_t = coef_part.astype(jnp.float32).transpose(2, 1, 0)[:, None, :, :]
    coef_mix = jnp.concatenate(
        [block_cos[None, :, None, :] * coef_t, -block_sin[None, :, None, :] * coef_t], axis=3
    )
    response = jnp.einsum(
        "ckrj,bj->ckrb", coef_mix, inner_tab,
        precision=lax.Precision.HIGHEST, preferred_element_type=jnp.float32,
    )
    prod_real = response[:, :, 0] * spec_gated[:, :, 0] + response[:, :, 1] * spec_gated[:, :, 1]
    prod_imag = response[:, :, 0] * spec_gated[:, :, 1] - response[:, :, 1] * spec_gated[:, :, 0]
    product = jnp.stack([prod_real, prod_imag], axis=2).astype(jnp.bfloat16)
    flat_product = product.reshape(width_share, nblocks, 2 * BLOCK)
    back_parts = jnp.einsum(
        "ckm,mj->ckj", flat_product, back_first, preferred_element_type=jnp.float32
    )
    back_parts = back_parts.reshape(width_share, nblocks, 2, BLOCK)
    back_twisted = twist_leading(back_parts, block_ids, all_inner, seq_total, 1.0).astype(
        jnp.bfloat16
    )
    time_field = jnp.einsum(
        "ckrm,krn->cnm", back_twisted, back_second, preferred_element_type=jnp.float32
    )
    time_field = time_field.reshape(width_share, seq_total).astype(jnp.bfloat16)
    time_field, normed_moved = lax.optimization_barrier((time_field, normed_moved))
    spec_normed = local_freq(normed_moved)
    grad_real = (
        spec_normed[:, :, 0] * spec_gated[:, :, 0] + spec_normed[:, :, 1] * spec_gated[:, :, 1]
    )
    grad_imag = (
        spec_normed[:, :, 0] * spec_gated[:, :, 1] - spec_normed[:, :, 1] * spec_gated[:, :, 0]
    )
    spec_grad = jnp.stack([grad_real, grad_imag], axis=2).astype(jnp.bfloat16)
    partial = jnp.einsum(
        "ckrb,bj->ckrj", spec_grad.astype(jnp.float32), inner_tab,
        precision=lax.Precision.HIGHEST, preferred_element_type=jnp.float32,
    )
    coef_local = jnp.sum(
        partial[..., :FEAT] * block_cos[None, :, None, :]
        - partial[..., FEAT:] * block_sin[None, :, None, :],
        axis=1,
    ).transpose(2, 1, 0)
    home_field = lax.all_to_all(time_field, "seq", split_axis=1, concat_axis=0, tiled=True)
    coef_local, home_field = lax.optimization_barrier((coef_local, home_field))
    coef_sum = lax.all_to_all(coef_local, "seq", split_axis=0, concat_axis=2, tiled=True)
    filter_grad = coef_sum / math.sqrt(seq_total)
    conv_grad = home_field.T.astype(jnp.float32)
    normed_grad = conv_grad + skip_weight[None, :] * gated.astype(jnp.float32)
    scaled_grad = gain[None, :] * normed_grad
    row_dot = taken_together(jnp.sum(scaled_grad * upcast, axis=1), "ch")
    hidden_grad = (
        inverse_rms[:, None] * scaled_grad - upcast * (inverse_rms**3 * row_dot / D)[:, None]
    )
    return (hidden_grad.astype(jnp.bfloat16), filter_grad)


def solution(mesh):
    in_specs = (P("seq", "ch"), P("seq", "ch"), P("ch"), P("ch"), P(None, None, "ch"), P())
    out_specs = (P("seq", "ch"), P("seq", None, "ch"))
    return jax.shard_map(
        per_device, mesh=mesh, in_specs=in_specs, out_specs=out_specs, check_vma=False
    )
```

profile of v0, /device:TPU:1, one launch (start us, length us, event | category | flops | bytes accessed | tf_op | source)
XLA Modules:
  0.0 167.9 jit_solution(10076024507030636643)
XLA Ops:
  0.6 1.5 copy.99
  2.4 3.3 %collective-permute-start = (f32[2048]{0:T(1024)S(1)}, f32[2048]{0:T(1024)S(1)}, u32[]{:S(2)}, u32[]{:S(2)}) collective-permute-start(f32[2048]{0:T(1024)S(1)} %fusion), channel_id=1, source_target_pairs={{0,1},{1,0},{2,3},{3,2},{4,5},{5,4},{6,7},{7,6},{8,9},{9,8},{10,11... | collective-permute-start | bytes 24584 | tf_op jit(solution)/shard_map/ppermute | solution.py:26
  8.6 2.3 %copy.98 = bf16[2048,256]{0,1:T(8,128)(2,1)} copy(bf16[2048,256]{1,0:T(8,128)(2,1)} %param.7) | data formatting | bytes 2097152 | tf_op args[1]
  10.8 2.3 %broadcast_select_fusion.2 = bf16[2048,256]{0,1:T(8,128)(2,1)} fusion(bf16[2048,256]{0,1:T(8,128)(2,1)} %copy.98, pred[2048]{0:T(1024)(128)(4,1)S(1)} %fusion.78), kind=kLoop, calls=%fused_computation.57 | loop fusion | flops 524288 | bytes 2099200 | tf_op jit(solution)/shard_map/jit(_where)/select_n | solution.py:100
  13.3 3.1 %broadcast_select_fusion = (bf16[2,512,512]{1,0,2:T(2,128)(2,1)S(1)}, bf16[2,512,512]{1,0,2:T(2,128)(2,1)S(1)}) fusion(pred[2]{0:T(512)(128)(4,1)S(1)} %iota_compare_fusion.1, bf16[512,512]{0,1:T(8,128)(2,1)S(1)} %get-tuple-element.60, f32[512,512]{0,1:T(8,128)S(1)} %bitcast.126, bf16[512,512]{0,1:T(8,128)(2,1)S(1)} %get-tuple-element.61, ...), kind=kLoop, calls=%fused_computation.38 | loop fusion | flops 1048576 | bytes 5242882 | tf_op jit(solution)/shard_map/jit(_where)/select_n | solution.py:51
  16.4 4.6 %select_convert_fusion = (bf16[2,512,2,512]{1,0,3,2:T(2,128)(2,1)S(1)}, bf16[2,512,2,512]{1,0,3,2:T(2,128)(2,1)}) fusion(pred[2,2]{0,1:T(4,128)(4,1)S(1)} %iota_compare_fusion, bf16[2,512,512]{1,0,2:T(2,128)(2,1)S(1)} %get-tuple-element.48, bf16[512,512]{0,1:T(8,128)(2,1)S(1)} %bitcast.140, bf16[2,512,512]{1,0,2:T(2,128)(2,1)S(1)} %get-tuple-element.49), kind=kLoop, calls=%fused_computation | loop fusion | flops 2097152 | bytes 6815748 | tf_op jit(solution)/shard_map/convert_element_type | solution.py:103
  22.1 1.7 %collective-permute-done.1 = f32[2048]{0:T(1024)S(1)} collective-permute-done((f32[2048]{0:T(1024)S(1)}, f32[2048]{0:T(1024)S(1)}, u32[]{:S(2)}, u32[]{:S(2)}) %collective-permute-start.1) | collective-permute-done | bytes 8224 | tf_op jit(solution)/shard_map/ppermute | solution.py:26
  25.6 3.5 %copy.139 = bf16[128,8,2,512]{3,1,2,0:T(8,128)(2,1)} copy(bf16[128,8,2,512]{3,2,1,0:T(2,128)(2,1)} %bitcast.131) | data formatting | bytes 4194304
  29.4 2.0 %copy.140 = bf16[128,8,2,512]{3,1,2,0:T(8,128)(2,1)} copy(bf16[128,8,2,512]{3,2,1,0:T(2,128)(2,1)S(1)} %bitcast.130) | data formatting | bytes 4194304
  32.1 11.4 %all-to-all-start = ((bf16[32,8,2048]{2,1,0:T(8,128)(2,1)}), bf16[32,8,2048]{2,1,0:T(8,128)(2,1)S(1)}, u32[]{:S(2)}, u32[]{:S(2)}) async-start(bf16[32,8,2048]{2,1,0:T(8,128)(2,1)} %bitcast.12), calls=%async_computation | async-start | bytes 2097152 | tf_op jit(solution)/shard_map/all_to_all | solution.py:110
  43.5 1.6 fusion.32
  46.9 5.1 %fusion.22 = f32[8,128,2,512]{3,1,2,0:T(8,128)} fusion(f32[8,128,2,64]{3,1,2,0:T(8,128)S(1)} %get-tuple-element.44, f32[8,128,2,64]{3,1,2,0:T(8,128)S(1)} %get-tuple-element.43, f32[512,64]{0,1:T(8,128)S(1)} %get-tuple-element.55, f32[512,64]{0,1:T(8,128)S(1)} %get-tuple-element.54), kind=kOutput, calls=%fused_computation.45 | convolution fusion | flops 1610940416 | bytes 5505024 | tf_op jit(solution)/shard_map/ckrj,bj->ckrb/dot_general | solution.py:134
  54.1 14.2 %all-to-all-done = bf16[32,8,2048]{2,1,0:T(8,128)(2,1)S(1)} async-done(((bf16[32,8,2048]{2,1,0:T(8,128)(2,1)}), bf16[32,8,2048]{2,1,0:T(8,128)(2,1)S(1)}, u32[]{:S(2)}, u32[]{:S(2)}) %all-to-all-start) | async-done | bytes 1048608 | tf_op jit(solution)/shard_map/all_to_all | solution.py:110
  70.2 2.4 %copy.105 = bf16[8,128,2,512]{1,3,2,0:T(8,128)(2,1)} copy(bf16[8,128,2,512]{3,1,0,2:T(8,128)(2,1)S(1)} %pad_maximum_fusion) | data formatting | bytes 4194304 | tf_op jit(solution)/shard_map/stack | solution.py:63
  72.7 8.6 %all-to-all-start.1 = ((bf16[32,8,2048]{2,1,0:T(8,128)(2,1)}), bf16[32,8,2048]{2,1,0:T(8,128)(2,1)}, u32[]{:S(2)}, u32[]{:S(2)}) async-start(bf16[32,8,2048]{2,1,0:T(8,128)(2,1)} %bitcast.132), calls=%async_computation.1 | async-start | bytes 2097152 | tf_op jit(solution)/shard_map/all_to_all | solution.py:112
  81.3 4.1 %fusion.94 = f32[8,128,2,512]{3,1,2,0:T(8,128)S(1)} fusion(bf16[8,128,1024,1]{1,2,3,0:T(8,128)(2,1)} %bitcast.137, bf16[2,512,1024,1]{2,1,0,3:T(8,128)(2,1)S(1)} %bitcast.135), kind=kOutput, calls=%fused_computation.164 | convolution fusion | flops 2147483648 | bytes 8388608 | tf_op jit(solution)/shard_map/ckm,mj->ckj/dot_general | solution.py:123
  87.7 2.4 %copy.107 = bf16[8,128,2,512]{1,3,2,0:T(8,128)(2,1)} copy(bf16[8,128,2,512]{3,1,2,0:T(8,128)(2,1)S(1)} %pad_maximum_fusion.1) | data formatting | bytes 4194304 | tf_op jit(solution)/shard_map/stack | solution.py:140
  90.1 4.6 %fusion.95 = f32[8,128,2,512]{3,1,0,2:T(8,128)S(1)} fusion(bf16[8,128,1024,1]{1,2,0,3:T(8,128)(2,1)} %bitcast.138, bf16[2,512,1024,1]{2,1,3,0:T(8,128)(2,1)} %bitcast.136), kind=kOutput, calls=%fused_computation.165 | convolution fusion | flops 2147483648 | bytes 8388608 | tf_op jit(solution)/shard_map/ckm,mj->ckj/dot_general | solution.py:142
  96.0 1.6 copy.141
  97.5 8.7 %all-to-all-done.1 = bf16[32,8,2048]{2,1,0:T(8,128)(2,1)} async-done(((bf16[32,8,2048]{2,1,0:T(8,128)(2,1)}), bf16[32,8,2048]{2,1,0:T(8,128)(2,1)}, u32[]{:S(2)}, u32[]{:S(2)}) %all-to-all-start.1) | async-done | bytes 1048608 | tf_op jit(solution)/shard_map/all_to_all | solution.py:112
  106.2 8.3 %all-to-all-start.2 = ((bf16[8,32,2048]{2,0,1:T(8,128)(2,1)}), bf16[8,32,2048]{2,0,1:T(8,128)(2,1)S(1)}, u32[]{:S(2)}, u32[]{:S(2)}) async-start(bf16[8,32,2048]{2,0,1:T(8,128)(2,1)} %bitcast.47), calls=%async_computation.2 | async-start | bytes 2097152 | tf_op jit(solution)/shard_map/all_to_all | solution.py:171
  114.5 2.2 %convolution_bitcast_fusion = f32[8,128,2,512]{3,1,0,2:T(8,128)S(1)} fusion(bf16[8,128,512]{2,0,1:T(8,128)(2,1)} %bitcast.39, bf16[128,128,1]{0,1,2:T(8,128)(2,1)S(1)} %bitcast.142, bf16[128,128,1]{0,1,2:T(8,128)(2,1)S(1)} %bitcast.145), kind=kOutput, calls=%fused_computation.6 | convolution fusion | flops 268566528 | bytes 5308416 | tf_op jit(solution)/shard_map/cnm,nkr->ckrm/dot_general | solution.py:118
  117.5 1.6 pad_maximum_fusion.2
  119.0 4.0 %copy.113 = bf16[8,128,2,512]{1,3,2,0:T(8,128)(2,1)} copy(bf16[8,128,2,512]{3,1,0,2:T(8,128)(2,1)} %pad_maximum_fusion.2) | data formatting | bytes 4194304 | tf_op jit(solution)/shard_map/stack | solution.py:63
  123.0 4.7 %fusion.96 = f32[8,128,2,512]{3,1,2,0:T(8,128)S(1)} fusion(bf16[8,128,1024,1]{1,2,3,0:T(8,128)(2,1)} %bitcast.139, bf16[2,512,1024,1]{2,1,0,3:T(8,128)(2,1)} %bitcast.134), kind=kOutput, calls=%fused_computation.166 | convolution fusion | flops 2147483648 | bytes 8388608 | tf_op jit(solution)/shard_map/ckm,mj->ckj/dot_general | solution.py:123
  129.1 1.8 %fusion.10 = f32[8,128,2,128]{3,1,2,0:T(8,128)S(1)} fusion(bf16[8,128,1,512]{3,1,2,0:T(8,128)(2,1)S(1)} %get-tuple-element.27, bf16[8,128,1,512]{3,1,2,0:T(8,128)(2,1)S(1)} %get-tuple-element.26, f32[512,64]{0,1:T(8,128)S(1)} %copy-done.11, f32[512,64]{0,1:T(8,128)S(1)} %copy-done.9), kind=kOutput, calls=%fused_computation.22 | convolution fusion | flops 1611726848 | bytes 3407872 | tf_op jit(solution)/shard_map/ckrb,bj->ckrj/dot_general | solution.py:162
  131.3 8.1 %all-to-all-done.2 = bf16[8,32,2048]{2,0,1:T(8,128)(2,1)S(1)} async-done(((bf16[8,32,2048]{2,0,1:T(8,128)(2,1)}), bf16[8,32,2048]{2,0,1:T(8,128)(2,1)S(1)}, u32[]{:S(2)}, u32[]{:S(2)}) %all-to-all-start.2) | async-done | bytes 1048608 | tf_op jit(solution)/shard_map/all_to_all | solution.py:171
  139.4 1.8 %fusion.3 = f32[2048]{0:T(1024)S(1)} fusion(bf16[2048,256]{0,1:T(8,128)(2,1)S(1)} %copy.99, bf16[2048,256]{0,1:T(8,128)(2,1)} %broadcast_select_fusion.2, bf16[256,2048]{1,0:T(8,128)(2,1)S(1)} %bitcast.128, f32[256]{0:T(256)S(1)} %copy-done.18, f32[256]{0:T(256)S(1)} %copy-done.17), kind=kLoop, calls=%fused_computation.11 | loop fusion | flops 4192256 | bytes 3155968 | tf_op jit(solution)/shard_map/reduce_sum | solution.py:178
  141.3 4.6 %collective-permute-start.3 = (f32[2048]{0:T(1024)S(1)}, f32[2048]{0:T(1024)S(1)}, u32[]{:S(2)}, u32[]{:S(2)}) collective-permute-start(f32[2048]{0:T(1024)S(1)} %fusion.3), channel_id=1, source_target_pairs={{0,1},{1,0},{2,3},{3,2},{4,5},{5,4},{6,7},{7,6},{8,9},{9,8},{10,11... | collective-permute-start | bytes 24584 | tf_op jit(solution)/shard_map/ppermute | solution.py:26
  147.2 13.3 %all_to_all.66 = f32[64,2,8]{2,1,0:T(2,128)S(1)} all-to-all(f32[64,2,8]{2,1,0:T(2,128)S(1)} %copy.118), channel_id=1, replica_groups=mesh['seq'=32,'ch'=8] {'seq'}, dimensions={0} | all-to-all | bytes 8192 | tf_op jit(solution)/shard_map/all_to_all | solution.py:173
  160.6 1.8 %collective-permute-start.5 = (f32[2048]{0:T(1024)S(1)}, f32[2048]{0:T(1024)S(1)}, u32[]{:S(2)}, u32[]{:S(2)}) collective-permute-start(f32[2048]{0:T(1024)S(1)} %add.262), channel_id=1, source_target_pairs={{0,4},{1,5},{2,6},{3,7},{4,0},{5,1},{6,2},{7,3},{8,12},{9,13},{10,... | collective-permute-start | bytes 24584 | tf_op jit(solution)/shard_map/ppermute | solution.py:26
  164.6 1.9 %fusion.5 = bf16[2048,256]{0,1:T(8,128)(2,1)S(1)} fusion(bf16[2048,256]{0,1:T(8,128)(2,1)S(1)} %copy.99, bf16[2048,256]{0,1:T(8,128)(2,1)} %broadcast_select_fusion.2, bf16[256,2048]{1,0:T(8,128)(2,1)S(1)} %bitcast.129, f32[2048]{0:T(1024)S(1)} %fusion.80, f32[256]{0:T(256)S(1)} %copy-done.18, f32[256]{0:T(256)S(1)} %copy-done.17, f32[2048]{0:T(1024)S(1)} %add_rsqrt_fusion), kind=kLoop, calls=%fused_computation.13 | loop fusion | flops 5242880 | bytes 4212736 | tf_op jit(solution)/shard_map/convert_element_type | solution.py:182
  (109 shorter events, 23.5 us)
Async XLA Ops:
  2.1 6.0 %copy-start.21 = (s32[64]{0:T(128)S(1)}, s32[64]{0:T(128)}, u32[]{:S(2)}) copy-start(s32[64]{0:T(128)} %param.11) | copy-start | bytes 772
  2.4 18.8 %collective-permute-start = (f32[2048]{0:T(1024)S(1)}, f32[2048]{0:T(1024)S(1)}, u32[]{:S(2)}, u32[]{:S(2)}) collective-permute-start(f32[2048]{0:T(1024)S(1)} %fusion), channel_id=1, source_target_pairs={{0,1},{1,0},{2,3},{3,2},{4,5},{5,4},{6,7},{7,6},{8,9},{9,8},{10,11... | collective-permute-start | bytes 24584 | tf_op jit(solution)/shard_map/ppermute | solution.py:26
  8.1 12.9 %copy-start.19 = (s32[64]{0:T(128)}, s32[64]{0:T(128)S(1)}, u32[]{:S(2)}) copy-start(s32[64]{0:T(128)S(1)} %multiply_add_fusion.2) | copy-start | bytes 772
  13.3 3.1 %copy-start.6 = (bf16[512,8,64]{0,2,1:T(8,128)(2,1)S(1)}, bf16[512,8,64]{0,2,1:T(8,128)(2,1)}, u32[]{:S(2)}) copy-start(bf16[512,8,64]{0,2,1:T(8,128)(2,1)} %subtract_multiply_fusion) | copy-start | bytes 1572868
  16.4 8.5 %copy-start.16 = (bf16[64,2,256]{2,1,0:T(2,128)(2,1)S(1)}, bf16[64,2,256]{2,1,0:T(2,128)(2,1)}, u32[]{:S(2)}) copy-start(bf16[64,2,256]{2,1,0:T(2,128)(2,1)} %param.10) | copy-start | bytes 196612
  16.4 8.6 %copy-start.22 = (bf16[256]{0:T(256)(128)(2,1)S(1)}, bf16[256]{0:T(256)(128)(2,1)}, u32[]{:S(2)}) copy-start(bf16[256]{0:T(256)(128)(2,1)} %param.8) | copy-start | bytes 1540
  21.2 2.6 %collective-permute-start.1 = (f32[2048]{0:T(1024)S(1)}, f32[2048]{0:T(1024)S(1)}, u32[]{:S(2)}, u32[]{:S(2)}) collective-permute-start(f32[2048]{0:T(1024)S(1)} %add.239), channel_id=1, source_target_pairs={{0,2},{1,3},{2,0},{3,1},{4,6},{5,7},{6,4},{7,5},{8,10},{9,11},{10,... | collective-permute-start | bytes 24584 | tf_op jit(solution)/shard_map/ppermute | solution.py:26
  23.8 8.2 %collective-permute-start.2 = (f32[2048]{0:T(1024)S(1)}, f32[2048]{0:T(1024)S(1)}, u32[]{:S(2)}, u32[]{:S(2)}) collective-permute-start(f32[2048]{0:T(1024)S(1)} %add.240), channel_id=1, source_target_pairs={{0,4},{1,5},{2,6},{3,7},{4,0},{5,1},{6,2},{7,3},{8,12},{9,13},{10,... | collective-permute-start | bytes 24584 | tf_op jit(solution)/shard_map/ppermute | solution.py:26
  31.3 14.7 %copy-start.20 = (s32[64]{0:T(128)S(1)}, s32[64]{0:T(128)}, u32[]{:S(2)}) copy-start(s32[64]{0:T(128)} %copy-done.19) | copy-start | bytes 772
  32.1 36.3 %all-to-all-start = ((bf16[32,8,2048]{2,1,0:T(8,128)(2,1)}), bf16[32,8,2048]{2,1,0:T(8,128)(2,1)S(1)}, u32[]{:S(2)}, u32[]{:S(2)}) async-start(bf16[32,8,2048]{2,1,0:T(8,128)(2,1)} %bitcast.12), calls=%async_computation | async-start | bytes 2097152 | tf_op jit(solution)/shard_map/all_to_all | solution.py:110
  46.1 23.2 %copy-start.3 = (f32[128,512]{1,0:T(8,128)}, f32[128,512]{1,0:T(8,128)S(1)}, u32[]{:S(2)}) copy-start(f32[128,512]{1,0:T(8,128)S(1)} %get-tuple-element.59) | copy-start | bytes 786436
  46.7 5.4 %copy-start.8 = (f32[512,64]{0,1:T(8,128)}, f32[512,64]{0,1:T(8,128)S(1)}, u32[]{:S(2)}) copy-start(f32[512,64]{0,1:T(8,128)S(1)} %get-tuple-element.54) | copy-start | bytes 393220
  46.7 5.4 %copy-start.10 = (f32[512,64]{0,1:T(8,128)}, f32[512,64]{0,1:T(8,128)S(1)}, u32[]{:S(2)}) copy-start(f32[512,64]{0,1:T(8,128)S(1)} %get-tuple-element.55) | copy-start | bytes 393220
  46.9 5.3 %copy-start.13 = (f32[128,64]{0,1:T(8,128)S(1)}, f32[128,64]{0,1:T(8,128)}, u32[]{:S(2)}) copy-start(f32[128,64]{0,1:T(8,128)} %get-tuple-element.56) | copy-start | bytes 98308
  46.9 5.3 %copy-start.14 = (f32[128,64]{0,1:T(8,128)S(1)}, f32[128,64]{0,1:T(8,128)}, u32[]{:S(2)}) copy-start(f32[128,64]{0,1:T(8,128)} %get-tuple-element.57) | copy-start | bytes 98308
  46.9 5.9 %copy-start.17 = (f32[256]{0:T(256)S(1)}, f32[256]{0:T(256)}, u32[]{:S(2)}) copy-start(f32[256]{0:T(256)} %convert_element_type.207) | copy-start | bytes 3076
  72.7 8.6 %copy-start.5 = (bf16[128,8,2,512]{3,1,2,0:T(8,128)(2,1)S(1)}, bf16[128,8,2,512]{3,1,2,0:T(8,128)(2,1)}, u32[]{:S(2)}) copy-start(bf16[128,8,2,512]{3,1,2,0:T(8,128)(2,1)} %copy.139) | copy-start | bytes 6291460
  72.7 33.5 %all-to-all-start.1 = ((bf16[32,8,2048]{2,1,0:T(8,128)(2,1)}), bf16[32,8,2048]{2,1,0:T(8,128)(2,1)}, u32[]{:S(2)}, u32[]{:S(2)}) async-start(bf16[32,8,2048]{2,1,0:T(8,128)(2,1)} %bitcast.132), calls=%async_computation.1 | async-start | bytes 2097152 | tf_op jit(solution)/shard_map/all_to_all | solution.py:112
  81.3 4.1 %copy-start.2 = (f32[8,128,2,512]{3,1,2,0:T(8,128)S(1)}, f32[8,128,2,512]{3,1,2,0:T(8,128)}, u32[]{:S(2)}) copy-start(f32[8,128,2,512]{3,1,2,0:T(8,128)} %fusion.22) | copy-start | bytes 12582916
  85.4 2.0 %copy-start = (f32[8,128,2,512]{3,1,2,0:T(8,128)}, f32[8,128,2,512]{3,1,2,0:T(8,128)S(1)}, u32[]{:S(2)}) copy-start(f32[8,128,2,512]{3,1,2,0:T(8,128)S(1)} %fusion.94) | copy-start | bytes 12582916
  90.1 4.6 %copy-start.7 = (f32[128,512]{1,0:T(8,128)S(1)}, f32[128,512]{1,0:T(8,128)}, u32[]{:S(2)}) copy-start(f32[128,512]{1,0:T(8,128)} %fusion.32) | copy-start | bytes 786436
  94.8 0.8 copy-start.15
  106.2 33.2 %all-to-all-start.2 = ((bf16[8,32,2048]{2,0,1:T(8,128)(2,1)}), bf16[8,32,2048]{2,0,1:T(8,128)(2,1)S(1)}, u32[]{:S(2)}, u32[]{:S(2)}) async-start(bf16[8,32,2048]{2,0,1:T(8,128)(2,1)} %bitcast.47), calls=%async_computation.2 | async-start | bytes 2097152 | tf_op jit(solution)/shard_map/all_to_all | solution.py:171
  114.5 2.2 %copy-start.4 = (f32[128,512]{1,0:T(8,128)S(1)}, f32[128,512]{1,0:T(8,128)}, u32[]{:S(2)}) copy-start(f32[128,512]{1,0:T(8,128)} %copy-done.3) | copy-start | bytes 786436
  123.0 4.8 %copy-start.1 = (f32[8,128,2,512]{3,1,2,0:T(8,128)S(1)}, f32[8,128,2,512]{3,1,2,0:T(8,128)}, u32[]{:S(2)}) copy-start(f32[8,128,2,512]{3,1,2,0:T(8,128)} %copy-done) | copy-start | bytes 12582916
  127.7 1.3 copy-start.9
  127.8 1.3 copy-start.11
  129.0 1.9 %copy-start.12 = (f32[128,64]{1,0:T(8,128)S(1)}, f32[128,64]{1,0:T(8,128)}, u32[]{:S(2)}) copy-start(f32[128,64]{1,0:T(8,128)} %copy.117) | copy-start | bytes 98308
  130.9 8.5 %copy-start.18 = (f32[256]{0:T(256)S(1)}, f32[256]{0:T(256)}, u32[]{:S(2)}) copy-start(f32[256]{0:T(256)} %param.9) | copy-start | bytes 3076
  141.3 5.5 %collective-permute-start.3 = (f32[2048]{0:T(1024)S(1)}, f32[2048]{0:T(1024)S(1)}, u32[]{:S(2)}, u32[]{:S(2)}) collective-permute-start(f32[2048]{0:T(1024)S(1)} %fusion.3), channel_id=1, source_target_pairs={{0,1},{1,0},{2,3},{3,2},{4,5},{5,4},{6,7},{7,6},{8,9},{9,8},{10,11... | collective-permute-start | bytes 24584 | tf_op jit(solution)/shard_map/ppermute | solution.py:26
  146.8 13.8 %collective-permute-start.4 = (f32[2048]{0:T(1024)S(1)}, f32[2048]{0:T(1024)S(1)}, u32[]{:S(2)}, u32[]{:S(2)}) collective-permute-start(f32[2048]{0:T(1024)S(1)} %add.261), channel_id=1, source_target_pairs={{0,2},{1,3},{2,0},{3,1},{4,6},{5,7},{6,4},{7,5},{8,10},{9,11},{10,... | collective-permute-start | bytes 24584 | tf_op jit(solution)/shard_map/ppermute | solution.py:26
  160.6 4.1 %collective-permute-start.5 = (f32[2048]{0:T(1024)S(1)}, f32[2048]{0:T(1024)S(1)}, u32[]{:S(2)}, u32[]{:S(2)}) collective-permute-start(f32[2048]{0:T(1024)S(1)} %add.262), channel_id=1, source_target_pairs={{0,4},{1,5},{2,6},{3,7},{4,0},{5,1},{6,2},{7,3},{8,12},{9,13},{10,... | collective-permute-start | bytes 24584 | tf_op jit(solution)/shard_map/ppermute | solution.py:26
where the time goes:
time: 170 us; the launch traced here: 168 us
  starting transfers between devices  39.4 us (23%)
  waiting for transfers between devices  35 us (21%)
  other arithmetic  31 us (18%)
  matrix products  24 us (14%)
  local copies, waits for them, and re-layouts  23.9 us (14%)
  blocking collectives  13.3 us (8%)
    all_to_all x1, waiting for transfers between devices, per_device(): lax.all_to_all(gated.T, 'seq', split_axis=0, concat_axis=1, tiled=True)  14.2 us
    all_to_all x1, blocking collectives, per_device(): lax.all_to_all(coef_local, 'seq', split_axis=0, concat_axis=2, tiled=True)  13.3 us
    unnamed x52, local copies, waits for them, and re-layouts  13 us
    all_to_all x1, starting transfers between devices, per_device(): lax.all_to_all(gated.T, 'seq', split_axis=0, concat_axis=1, tiled=True)  11.4 us
    ppermute x6, starting transfers between devices, taken_together(): value = value + lax.ppermute(value, axis, pairs)  11.2 us
    dot_general x2, matrix products, local_freq(): jnp.einsum('ckm,mj->ckj', flat, forward_second, preferred_element_type=jn...  8.87 us
    all_to_all x1, waiting for transfers between devices, per_device(): lax.all_to_all(normed.T, 'seq', split_axis=0, concat_axis=1, tiled=True)  8.68 us
    all_to_all x1, starting transfers between devices, per_device(): lax.all_to_all(normed.T, 'seq', split_axis=0, concat_axis=1, tiled=True)  8.6 us
  transfers between devices with their start and end apart: 9, of which 6 were waited for; matrix products, arithmetic and copies ran while one was open for 40% of the time, Pallas kernels for 0%

commit v1 on v0

--- a/solution.py
+++ b/solution.py
@@ -100,7 +100,6 @@
     gated = jnp.where(keep[:, None], grad_out, jnp.zeros_like(grad_out))
     forward_first = jnp.stack(twin_table(nblocks, -1.0), axis=2).astype(jnp.bfloat16)
     forward_second = block_matrix(BLOCK, -1.0).astype(jnp.bfloat16)
-    back_first = block_matrix(BLOCK, 1.0).astype(jnp.bfloat16)
     cosine, sine_part = twin_table(nblocks, 1.0)
     back_second = jnp.stack([cosine, -sine_part], axis=1).astype(jnp.bfloat16)
     block_ids = jnp.arange(nblocks, dtype=jnp.int32)
@@ -140,7 +139,7 @@
     product = jnp.stack([prod_real, prod_imag], axis=2).astype(jnp.bfloat16)
     flat_product = product.reshape(width_share, nblocks, 2 * BLOCK)
     back_parts = jnp.einsum(
-        "ckm,mj->ckj", flat_product, back_first, preferred_element_type=jnp.float32
+        "ckm,jm->ckj", flat_product, forward_second, preferred_element_type=jnp.float32
     )
     back_parts = back_parts.reshape(width_share, nblocks, 2, BLOCK)
     back_twisted = twist_leading(back_parts, block_ids, all_inner, seq_total, 1.0).astype(

time: 170 us -> 173 us (1.018)
  local copies, waits for them, and re-layouts: 23.9 us -> 28.6 us
    dot_general x0 -> x1, local copies, waits for them, and re-layouts: none -> 3.96 us  [local_freq(): jnp.einsum('ckm,mj->ckj', flat, forward_second, preferred_element_type=jn...]
    select_n x1, other arithmetic: 3.06 us -> 0.17 us  [block_matrix(): jnp.where(upper, sine_part[None, :, None, :], -sine_part[None, :, None, :])]
    convert_element_type x1 -> x2, other arithmetic: 4.58 us -> 7.2 us  [per_device(): forward_second = block_matrix(BLOCK, -1.0).astype(jnp.bfloat16)]
    another operation x2 -> x1, local copies, waits for them, and re-layouts: 2.54 us -> 0.1 us  [the longest x1 2.44 us: per_device(): product = jnp.stack([prod_real, prod_imag], axis=2).astype(jnp.bfloat16)]
    dot_general x1, matrix products: 4.64 us -> 2.36 us  [per_device(): jnp.einsum('ckm,jm->ckj', flat_product, forward_second, preferred_element...]
    mul x0 -> x2, local copies, waits for them, and re-layouts: none -> 2.27 us  [twin_table(): return (cosine * factor, sign * sine * factor)]
    all_to_all x1, waiting for transfers between devices: 8.68 us -> 6.47 us  [per_device(): lax.all_to_all(normed.T, 'seq', split_axis=0, concat_axis=1, tiled=True)]
    neg x0 -> x1, local copies, waits for them, and re-layouts: none -> 2.07 us  [block_matrix(): -sine_part[None, :, None, :]]
  transfers between devices with their start and end apart: 9 -> 9, of which waited for: 6 -> 6; matrix products, arithmetic and copies ran while one was open for 40% -> 43% of each run, Pallas kernels for 0% -> 0%
where the time goes in v1:
time: 173 us; the launch traced here: 171 us
  starting transfers between devices  39.3 us (23%)
  waiting for transfers between devices  33.4 us (19%)
  other arithmetic  31.2 us (18%)
  local copies, waits for them, and re-layouts  28.6 us (17%)
  matrix products  23.6 us (14%)
  blocking collectives  13.3 us (8%)
    all_to_all x1, waiting for transfers between devices, per_device(): lax.all_to_all(gated.T, 'seq', split_axis=0, concat_axis=1, tiled=True)  14.1 us
    all_to_all x1, blocking collectives, per_device(): lax.all_to_all(coef_local, 'seq', split_axis=0, concat_axis=2, tiled=True)  13.3 us
    unnamed x51, local copies, waits for them, and re-layouts  11.8 us
    all_to_all x1, starting transfers between devices, per_device(): lax.all_to_all(gated.T, 'seq', split_axis=0, concat_axis=1, tiled=True)  11.5 us
    ppermute x6, starting transfers between devices, taken_together(): value = value + lax.ppermute(value, axis, pairs)  11.2 us
    dot_general x2, matrix products, local_freq(): jnp.einsum('ckm,mj->ckj', flat, forward_second, preferred_element_type=jn...  9.49 us
    all_to_all x1, starting transfers between devices, per_device(): lax.all_to_all(normed.T, 'seq', split_axis=0, concat_axis=1, tiled=True)  8.43 us
    all_to_all x1, starting transfers between devices, per_device(): lax.all_to_all(time_field, 'seq', split_axis=1, concat_axis=0, tiled=True)  8.25 us
  transfers between devices with their start and end apart: 9, of which 6 were waited for; matrix products, arithmetic and copies ran while one was open for 43% of the time, Pallas kernels for 0%

profile of v1, /device:TPU:1, one launch (start us, length us, event | category | flops | bytes accessed | tf_op | source)
XLA Modules:
  0.0 170.5 jit_solution(8858398042943161910)
XLA Ops:
  0.6 1.5 copy.109
  2.4 3.3 %collective-permute-start = (f32[2048]{0:T(1024)S(1)}, f32[2048]{0:T(1024)S(1)}, u32[]{:S(2)}, u32[]{:S(2)}) collective-permute-start(f32[2048]{0:T(1024)S(1)} %fusion), channel_id=1, source_target_pairs={{0,1},{1,0},{2,3},{3,2},{4,5},{5,4},{6,7},{7,6},{8,9},{9,8},{10,11... | collective-permute-start | bytes 24584 | tf_op jit(solution)/shard_map/ppermute | solution.py:26
  5.7 1.6 fusion.34
  12.3 1.6 fusion.33
  16.7 2.1 %copy.118 = bf16[512,512]{1,0:T(8,128)(2,1)} copy(bf16[512,512]{0,1:T(8,128)(2,1)} %bitcast_negate_fusion) | data formatting | bytes 1048576 | tf_op jit(solution)/shard_map/neg | solution.py:51
  22.8 3.6 %select_convert_fusion = bf16[2,512,2,512]{3,2,1,0:T(2,128)(2,1)} fusion(pred[2,2]{1,0:T(4,128)(4,1)S(1)} %copy-done.18, bf16[2,512,512]{2,1,0:T(8,128)(2,1)S(1)} %broadcast_select_fusion, bf16[512,512]{1,0:T(8,128)(2,1)S(1)} %copy.116), kind=kLoop, calls=%fused_computation | loop fusion | flops 1048576 | bytes 3670020 | tf_op jit(solution)/shard_map/convert_element_type | solution.py:102
  26.8 2.4 %collective-permute-done.1 = f32[2048]{0:T(1024)S(1)} collective-permute-done((f32[2048]{0:T(1024)S(1)}, f32[2048]{0:T(1024)S(1)}, u32[]{:S(2)}, u32[]{:S(2)}) %collective-permute-start.1) | collective-permute-done | bytes 8224 | tf_op jit(solution)/shard_map/ppermute | solution.py:26
  30.3 3.5 %copy.156 = bf16[128,8,2,512]{3,1,2,0:T(8,128)(2,1)} copy(bf16[128,8,2,512]{3,2,1,0:T(2,128)(2,1)} %bitcast.116) | data formatting | bytes 4194304
  33.8 4.0 %copy.155 = bf16[1024,1024]{1,0:T(8,128)(2,1)} copy(bf16[1024,1024]{0,1:T(8,128)(2,1)} %bitcast.117) | data formatting | bytes 4194304 | tf_op jit(solution)/shard_map/ckm,mj->ckj/dot_general | solution.py:122
  38.8 11.5 %all-to-all-start = ((bf16[32,8,2048]{2,1,0:T(8,128)(2,1)}), bf16[32,8,2048]{2,1,0:T(8,128)(2,1)}, u32[]{:S(2)}, u32[]{:S(2)}) async-start(bf16[32,8,2048]{2,1,0:T(8,128)(2,1)} %bitcast.12), calls=%async_computation | async-start | bytes 2097152 | tf_op jit(solution)/shard_map/all_to_all | solution.py:109
  50.5 5.1 %fusion.25 = f32[8,128,2,512]{3,1,2,0:T(8,128)} fusion(f32[8,128,2,64]{3,1,2,0:T(8,128)S(1)} %get-tuple-element.40, f32[8,128,2,64]{3,1,2,0:T(8,128)S(1)} %get-tuple-element.39, f32[512,64]{0,1:T(8,128)S(1)} %copy-done.11, f32[512,64]{0,1:T(8,128)S(1)} %copy-done.9), kind=kOutput, calls=%fused_computation.46 | convolution fusion | flops 1610940416 | bytes 5505024 | tf_op jit(solution)/shard_map/ckrj,bj->ckrb/dot_general | solution.py:133
  56.3 3.6 %fusion.102 = bf16[2,512,2,512,1]{3,2,1,0,4:T(2,128)(2,1)} fusion(bf16[2,512,512]{2,1,0:T(8,128)(2,1)S(1)} %broadcast_select_fusion, bf16[512,512]{1,0:T(8,128)(2,1)S(1)} %copy.116, pred[2,2]{1,0:T(4,128)(4,1)S(1)} %copy-done.19), kind=kLoop, calls=%fused_computation.166 | loop fusion | flops 1048576 | bytes 3670020 | tf_op jit(solution)/shard_map/convert_element_type | solution.py:102
  61.2 14.1 %all-to-all-done = bf16[32,8,2048]{2,1,0:T(8,128)(2,1)} async-done(((bf16[32,8,2048]{2,1,0:T(8,128)(2,1)}), bf16[32,8,2048]{2,1,0:T(8,128)(2,1)}, u32[]{:S(2)}, u32[]{:S(2)}) %all-to-all-start) | async-done | bytes 1048608 | tf_op jit(solution)/shard_map/all_to_all | solution.py:109
  75.3 8.4 %all-to-all-start.1 = ((bf16[32,8,2048]{2,1,0:T(8,128)(2,1)}), bf16[32,8,2048]{2,1,0:T(8,128)(2,1)}, u32[]{:S(2)}, u32[]{:S(2)}) async-start(bf16[32,8,2048]{2,1,0:T(8,128)(2,1)} %bitcast.33), calls=%async_computation.1 | async-start | bytes 2097152 | tf_op jit(solution)/shard_map/all_to_all | solution.py:111
  83.7 2.2 %convolution_bitcast_fusion.2 = f32[8,128,2,512]{3,1,0,2:T(8,128)S(1)} fusion(bf16[8,128,512]{2,0,1:T(8,128)(2,1)} %bitcast.15, bf16[128,128,1]{0,1,2:T(8,128)(2,1)S(1)} %bitcast.123, bf16[128,128,1]{0,1,2:T(8,128)(2,1)S(1)} %bitcast.125), kind=kOutput, calls=%fused_computation.7 | convolution fusion | flops 268566528 | bytes 5308416 | tf_op jit(solution)/shard_map/cnm,nkr->ckrm/dot_general | solution.py:117
  86.9 2.5 %copy.115 = bf16[8,128,2,512]{1,3,2,0:T(8,128)(2,1)} copy(bf16[8,128,2,512]{3,1,0,2:T(8,128)(2,1)S(1)} %pad_maximum_fusion) | data formatting | bytes 4194304 | tf_op jit(solution)/shard_map/stack | solution.py:63
  89.4 4.7 %fusion.96 = f32[8,128,2,512]{3,1,2,0:T(8,128)S(1)} fusion(bf16[8,128,1024,1]{1,2,3,0:T(8,128)(2,1)} %bitcast.121, bf16[2,512,1024,1]{2,1,0,3:T(8,128)(2,1)} %bitcast.118), kind=kOutput, calls=%fused_computation.164 | convolution fusion | flops 2147483648 | bytes 8388608 | tf_op jit(solution)/shard_map/ckm,mj->ckj/dot_general | solution.py:122
  97.2 2.4 %convolution_bitcast_fusion.1 = f32[8,128,2,512]{3,1,0,2:T(8,128)S(1)} fusion(bf16[8,128,1,512]{3,1,2,0:T(8,128)(2,1)S(1)} %get-tuple-element.29, bf16[8,128,1,512]{3,1,2,0:T(8,128)(2,1)S(1)} %get-tuple-element.28, bf16[2,512,2,512,1]{3,2,1,0,4:T(2,128)(2,1)S(1)} %copy-done.7), kind=kOutput, calls=%fused_computation.6 | convolution fusion | flops 2151677952 | bytes 8388608 | tf_op jit(solution)/shard_map/ckm,jm->ckj/dot_general | solution.py:141
  100.8 1.6 copy.157
  102.4 6.5 %all-to-all-done.1 = bf16[32,8,2048]{2,1,0:T(8,128)(2,1)} async-done(((bf16[32,8,2048]{2,1,0:T(8,128)(2,1)}), bf16[32,8,2048]{2,1,0:T(8,128)(2,1)}, u32[]{:S(2)}, u32[]{:S(2)}) %all-to-all-start.1) | async-done | bytes 1048608 | tf_op jit(solution)/shard_map/all_to_all | solution.py:111
  108.9 8.2 %all-to-all-start.2 = ((bf16[8,32,2048]{2,0,1:T(8,128)(2,1)}), bf16[8,32,2048]{2,0,1:T(8,128)(2,1)S(1)}, u32[]{:S(2)}, u32[]{:S(2)}) async-start(bf16[8,32,2048]{2,0,1:T(8,128)(2,1)} %bitcast.45), calls=%async_computation.2 | async-start | bytes 2097152 | tf_op jit(solution)/shard_map/all_to_all | solution.py:170
  117.1 2.2 %convolution_bitcast_fusion = f32[8,128,2,512]{3,1,0,2:T(8,128)S(1)} fusion(bf16[8,128,512]{2,0,1:T(8,128)(2,1)} %bitcast.36, bf16[128,128,1]{0,1,2:T(8,128)(2,1)S(1)} %bitcast.124, bf16[128,128,1]{0,1,2:T(8,128)(2,1)S(1)} %bitcast.127), kind=kOutput, calls=%fused_computation.5 | convolution fusion | flops 268566528 | bytes 5308416 | tf_op jit(solution)/shard_map/cnm,nkr->ckrm/dot_general | solution.py:117
  120.1 1.6 pad_maximum_fusion.1
  121.6 4.0 %copy.126 = bf16[8,128,2,512]{1,3,2,0:T(8,128)(2,1)} copy(bf16[8,128,2,512]{3,1,0,2:T(8,128)(2,1)} %pad_maximum_fusion.1) | data formatting | bytes 4194304 | tf_op jit(solution)/shard_map/stack | solution.py:63
  125.6 4.7 %fusion.97 = f32[8,128,2,512]{3,1,2,0:T(8,128)S(1)} fusion(bf16[8,128,1024,1]{1,2,3,0:T(8,128)(2,1)} %bitcast.120, bf16[2,512,1024,1]{2,1,0,3:T(8,128)(2,1)} %bitcast.119), kind=kOutput, calls=%fused_computation.165 | convolution fusion | flops 2147483648 | bytes 8388608 | tf_op jit(solution)/shard_map/ckm,mj->ckj/dot_general | solution.py:122
  131.7 1.8 %fusion.12 = f32[8,128,2,128]{3,1,2,0:T(8,128)S(1)} fusion(bf16[8,128,1,512]{3,1,2,0:T(8,128)(2,1)S(1)} %get-tuple-element.27, bf16[8,128,1,512]{3,1,2,0:T(8,128)(2,1)S(1)} %get-tuple-element.26, f32[512,64]{0,1:T(8,128)S(1)} %copy-done.12, f32[512,64]{0,1:T(8,128)S(1)} %copy-done.10), kind=kOutput, calls=%fused_computation.24 | convolution fusion | flops 1611726848 | bytes 3407872 | tf_op jit(solution)/shard_map/ckrb,bj->ckrj/dot_general | solution.py:161
  133.9 8.1 %all-to-all-done.2 = bf16[8,32,2048]{2,0,1:T(8,128)(2,1)S(1)} async-done(((bf16[8,32,2048]{2,0,1:T(8,128)(2,1)}), bf16[8,32,2048]{2,0,1:T(8,128)(2,1)S(1)}, u32[]{:S(2)}, u32[]{:S(2)}) %all-to-all-start.2) | async-done | bytes 1048608 | tf_op jit(solution)/shard_map/all_to_all | solution.py:170
  142.1 1.8 %fusion.3 = f32[2048]{0:T(1024)S(1)} fusion(bf16[2048,256]{0,1:T(8,128)(2,1)S(1)} %copy.109, bf16[2048,256]{0,1:T(8,128)(2,1)} %broadcast_select_fusion.1, bf16[256,2048]{1,0:T(8,128)(2,1)S(1)} %bitcast.114, f32[256]{0:T(256)S(1)} %copy-done.17, f32[256]{0:T(256)S(1)} %convert_element_type.195), kind=kLoop, calls=%fused_computation.11 | loop fusion | flops 4192256 | bytes 3155968 | tf_op jit(solution)/shard_map/reduce_sum | solution.py:177
  143.9 4.6 %collective-permute-start.3 = (f32[2048]{0:T(1024)S(1)}, f32[2048]{0:T(1024)S(1)}, u32[]{:S(2)}, u32[]{:S(2)}) collective-permute-start(f32[2048]{0:T(1024)S(1)} %fusion.3), channel_id=1, source_target_pairs={{0,1},{1,0},{2,3},{3,2},{4,5},{5,4},{6,7},{7,6},{8,9},{9,8},{10,11... | collective-permute-start | bytes 24584 | tf_op jit(solution)/shard_map/ppermute | solution.py:26
  149.8 13.3 %all_to_all.66 = f32[64,2,8]{2,1,0:T(2,128)S(1)} all-to-all(f32[64,2,8]{2,1,0:T(2,128)S(1)} %copy.132), channel_id=1, replica_groups=mesh['seq'=32,'ch'=8] {'seq'}, dimensions={0} | all-to-all | bytes 8192 | tf_op jit(solution)/shard_map/all_to_all | solution.py:172
  163.2 1.8 %collective-permute-start.5 = (f32[2048]{0:T(1024)S(1)}, f32[2048]{0:T(1024)S(1)}, u32[]{:S(2)}, u32[]{:S(2)}) collective-permute-start(f32[2048]{0:T(1024)S(1)} %add.251), channel_id=1, source_target_pairs={{0,4},{1,5},{2,6},{3,7},{4,0},{5,1},{6,2},{7,3},{8,12},{9,13},{10,... | collective-permute-start | bytes 24584 | tf_op jit(solution)/shard_map/ppermute | solution.py:26
  167.3 1.9 %fusion.5 = bf16[2048,256]{0,1:T(8,128)(2,1)S(1)} fusion(bf16[2048,256]{0,1:T(8,128)(2,1)S(1)} %copy.109, bf16[2048,256]{0,1:T(8,128)(2,1)} %broadcast_select_fusion.1, bf16[256,2048]{1,0:T(8,128)(2,1)S(1)} %bitcast.115, f32[2048]{0:T(1024)S(1)} %fusion.81, f32[256]{0:T(256)S(1)} %copy-done.17, f32[256]{0:T(256)S(1)} %convert_element_type.195, ...), kind=kLoop, calls=%fused_computation.13 | loop fusion | flops 5242880 | bytes 4212736 | tf_op jit(solution)/shard_map/convert_element_type | solution.py:181
  (110 shorter events, 29.2 us)
Async XLA Ops:
  2.1 11.8 %copy-start.20 = (s32[64]{0:T(128)S(1)}, s32[64]{0:T(128)}, u32[]{:S(2)}) copy-start(s32[64]{0:T(128)} %param.11) | copy-start | bytes 772
  2.4 24.2 %collective-permute-start = (f32[2048]{0:T(1024)S(1)}, f32[2048]{0:T(1024)S(1)}, u32[]{:S(2)}, u32[]{:S(2)}) collective-permute-start(f32[2048]{0:T(1024)S(1)} %fusion), channel_id=1, source_target_pairs={{0,1},{1,0},{2,3},{3,2},{4,5},{5,4},{6,7},{7,6},{8,9},{9,8},{10,11... | collective-permute-start | bytes 24584 | tf_op jit(solution)/shard_map/ppermute | solution.py:26
  18.8 3.4 %copy-start.21 = (pred[2]{0:T(512)(128)(4,1)S(1)}, pred[2]{0:T(512)(128)(4,1)}, u32[]{:S(2)}) copy-start(pred[2]{0:T(512)(128)(4,1)} %iota_compare_fusion.1) | copy-start | bytes 10
  21.1 1.1 copy-start.5
  21.1 1.6 copy-start.6
  21.1 1.7 %copy-start.18 = (pred[2,2]{1,0:T(4,128)(4,1)S(1)}, pred[2,2]{1,0:T(4,128)(4,1)}, u32[]{:S(2)}) copy-start(pred[2,2]{1,0:T(4,128)(4,1)} %iota_compare_fusion) | copy-start | bytes 16
  22.8 3.9 %copy-start.16 = (bf16[64,2,256]{2,1,0:T(2,128)(2,1)S(1)}, bf16[64,2,256]{2,1,0:T(2,128)(2,1)}, u32[]{:S(2)}) copy-start(bf16[64,2,256]{2,1,0:T(2,128)(2,1)} %param.10) | copy-start | bytes 196612
  22.8 7.4 %copy-start.22 = (bf16[256]{0:T(256)(128)(2,1)S(1)}, bf16[256]{0:T(256)(128)(2,1)}, u32[]{:S(2)}) copy-start(bf16[256]{0:T(256)(128)(2,1)} %param.8) | copy-start | bytes 1540
  26.6 2.6 %collective-permute-start.1 = (f32[2048]{0:T(1024)S(1)}, f32[2048]{0:T(1024)S(1)}, u32[]{:S(2)}, u32[]{:S(2)}) collective-permute-start(f32[2048]{0:T(1024)S(1)} %add.228), channel_id=1, source_target_pairs={{0,2},{1,3},{2,0},{3,1},{4,6},{5,7},{6,4},{7,5},{8,10},{9,11},{10,... | collective-permute-start | bytes 24584 | tf_op jit(solution)/shard_map/ppermute | solution.py:26
  29.2 9.5 %collective-permute-start.2 = (f32[2048]{0:T(1024)S(1)}, f32[2048]{0:T(1024)S(1)}, u32[]{:S(2)}, u32[]{:S(2)}) collective-permute-start(f32[2048]{0:T(1024)S(1)} %add.229), channel_id=1, source_target_pairs={{0,4},{1,5},{2,6},{3,7},{4,0},{5,1},{6,2},{7,3},{8,12},{9,13},{10,... | collective-permute-start | bytes 24584 | tf_op jit(solution)/shard_map/ppermute | solution.py:26
  33.8 4.0 %copy-start.14 = (f32[128,64]{0,1:T(8,128)S(1)}, f32[128,64]{0,1:T(8,128)}, u32[]{:S(2)}) copy-start(f32[128,64]{0,1:T(8,128)} %get-tuple-element.43) | copy-start | bytes 98308
  38.7 11.7 %copy-start.9 = (f32[512,64]{0,1:T(8,128)S(1)}, f32[512,64]{0,1:T(8,128)}, u32[]{:S(2)}) copy-start(f32[512,64]{0,1:T(8,128)} %get-tuple-element.48) | copy-start | bytes 393220
  38.8 11.7 %copy-start.11 = (f32[512,64]{0,1:T(8,128)S(1)}, f32[512,64]{0,1:T(8,128)}, u32[]{:S(2)}) copy-start(f32[512,64]{0,1:T(8,128)} %get-tuple-element.49) | copy-start | bytes 393220
  38.8 36.5 %all-to-all-start = ((bf16[32,8,2048]{2,1,0:T(8,128)(2,1)}), bf16[32,8,2048]{2,1,0:T(8,128)(2,1)}, u32[]{:S(2)}, u32[]{:S(2)}) async-start(bf16[32,8,2048]{2,1,0:T(8,128)(2,1)} %bitcast.12), calls=%async_computation | async-start | bytes 2097152 | tf_op jit(solution)/shard_map/all_to_all | solution.py:109
  50.5 5.8 %copy-start.19 = (pred[2,2]{1,0:T(4,128)(4,1)S(1)}, pred[2,2]{1,0:T(4,128)(4,1)}, u32[]{:S(2)}) copy-start(pred[2,2]{1,0:T(4,128)(4,1)} %iota_compare_fusion) | copy-start | bytes 16
  75.3 33.6 %all-to-all-start.1 = ((bf16[32,8,2048]{2,1,0:T(8,128)(2,1)}), bf16[32,8,2048]{2,1,0:T(8,128)(2,1)}, u32[]{:S(2)}, u32[]{:S(2)}) async-start(bf16[32,8,2048]{2,1,0:T(8,128)(2,1)} %bitcast.33), calls=%async_computation.1 | async-start | bytes 2097152 | tf_op jit(solution)/shard_map/all_to_all | solution.py:111
  83.7 2.2 %copy-start.3 = (f32[128,512]{1,0:T(8,128)S(1)}, f32[128,512]{1,0:T(8,128)}, u32[]{:S(2)}) copy-start(f32[128,512]{1,0:T(8,128)} %get-tuple-element.53) | copy-start | bytes 786436
  89.4 4.8 %copy-start.2 = (f32[8,128,2,512]{3,1,2,0:T(8,128)S(1)}, f32[8,128,2,512]{3,1,2,0:T(8,128)}, u32[]{:S(2)}) copy-start(f32[8,128,2,512]{3,1,2,0:T(8,128)} %fusion.25) | copy-start | bytes 12582916
  94.1 2.3 %copy-start = (f32[8,128,2,512]{3,1,2,0:T(8,128)}, f32[8,128,2,512]{3,1,2,0:T(8,128)S(1)}, u32[]{:S(2)}) copy-start(f32[8,128,2,512]{3,1,2,0:T(8,128)S(1)} %fusion.96) | copy-start | bytes 12582916
  94.1 3.1 %copy-start.7 = (bf16[2,512,2,512,1]{3,2,1,0,4:T(2,128)(2,1)S(1)}, bf16[2,512,2,512,1]{3,2,1,0,4:T(2,128)(2,1)}, u32[]{:S(2)}) copy-start(bf16[2,512,2,512,1]{3,2,1,0,4:T(2,128)(2,1)} %fusion.102) | copy-start | bytes 6291460
  97.2 2.4 %copy-start.8 = (f32[128,512]{1,0:T(8,128)S(1)}, f32[128,512]{1,0:T(8,128)}, u32[]{:S(2)}) copy-start(f32[128,512]{1,0:T(8,128)} %fusion.33) | copy-start | bytes 786436
  99.6 0.8 copy-start.15
  108.9 33.2 %all-to-all-start.2 = ((bf16[8,32,2048]{2,0,1:T(8,128)(2,1)}), bf16[8,32,2048]{2,0,1:T(8,128)(2,1)S(1)}, u32[]{:S(2)}, u32[]{:S(2)}) async-start(bf16[8,32,2048]{2,0,1:T(8,128)(2,1)} %bitcast.45), calls=%async_computation.2 | async-start | bytes 2097152 | tf_op jit(solution)/shard_map/all_to_all | solution.py:170
  117.1 2.2 %copy-start.4 = (f32[128,512]{1,0:T(8,128)S(1)}, f32[128,512]{1,0:T(8,128)}, u32[]{:S(2)}) copy-start(f32[128,512]{1,0:T(8,128)} %get-tuple-element.53) | copy-start | bytes 786436
  125.6 4.8 %copy-start.1 = (f32[8,128,2,512]{3,1,2,0:T(8,128)S(1)}, f32[8,128,2,512]{3,1,2,0:T(8,128)}, u32[]{:S(2)}) copy-start(f32[8,128,2,512]{3,1,2,0:T(8,128)} %copy-done) | copy-start | bytes 12582916
  130.4 1.3 copy-start.10
  130.4 1.3 copy-start.12
  131.6 1.9 %copy-start.13 = (f32[128,64]{1,0:T(8,128)S(1)}, f32[128,64]{1,0:T(8,128)}, u32[]{:S(2)}) copy-start(f32[128,64]{1,0:T(8,128)} %copy.131) | copy-start | bytes 98308
  133.5 8.5 %copy-start.17 = (f32[256]{0:T(256)S(1)}, f32[256]{0:T(256)}, u32[]{:S(2)}) copy-start(f32[256]{0:T(256)} %param.9) | copy-start | bytes 3076
  143.9 5.5 %collective-permute-start.3 = (f32[2048]{0:T(1024)S(1)}, f32[2048]{0:T(1024)S(1)}, u32[]{:S(2)}, u32[]{:S(2)}) collective-permute-start(f32[2048]{0:T(1024)S(1)} %fusion.3), channel_id=1, source_target_pairs={{0,1},{1,0},{2,3},{3,2},{4,5},{5,4},{6,7},{7,6},{8,9},{9,8},{10,11... | collective-permute-start | bytes 24584 | tf_op jit(solution)/shard_map/ppermute | solution.py:26
  149.4 13.8 %collective-permute-start.4 = (f32[2048]{0:T(1024)S(1)}, f32[2048]{0:T(1024)S(1)}, u32[]{:S(2)}, u32[]{:S(2)}) collective-permute-start(f32[2048]{0:T(1024)S(1)} %add.250), channel_id=1, source_target_pairs={{0,2},{1,3},{2,0},{3,1},{4,6},{5,7},{6,4},{7,5},{8,10},{9,11},{10,... | collective-permute-start | bytes 24584 | tf_op jit(solution)/shard_map/ppermute | solution.py:26
  163.2 4.1 %collective-permute-start.5 = (f32[2048]{0:T(1024)S(1)}, f32[2048]{0:T(1024)S(1)}, u32[]{:S(2)}, u32[]{:S(2)}) collective-permute-start(f32[2048]{0:T(1024)S(1)} %add.251), channel_id=1, source_target_pairs={{0,4},{1,5},{2,6},{3,7},{4,0},{5,1},{6,2},{7,3},{8,12},{9,13},{10,... | collective-permute-start | bytes 24584 | tf_op jit(solution)/shard_map/ppermute | solution.py:26

commit v2 on v0

--- a/solution.py
+++ b/solution.py
@@ -20,11 +20,11 @@
 
 def taken_together(value, axis):
     count = lax.axis_size(axis)
-    step = 1
-    while step < count:
+    step = count // 2
+    while step >= 1:
         pairs = [(i, i ^ step) for i in range(count)]
         value = value + lax.ppermute(value, axis, pairs)
-        step *= 2
+        step //= 2
     return value
 
 

time: 170 us -> 173 us (1.018)
  blocking collectives: 13.3 us -> 16.7 us
    all_to_all x1, blocking collectives: 13.3 us -> 16.7 us  [per_device(): lax.all_to_all(coef_local, 'seq', split_axis=0, concat_axis=2, tiled=True)]
  transfers between devices with their start and end apart: 9 -> 9, of which waited for: 6 -> 5; matrix products, arithmetic and copies ran while one was open for 40% -> 39% of each run, Pallas kernels for 0% -> 0%
where the time goes in v2:
time: 173 us; the launch traced here: 172 us
  starting transfers between devices  39.3 us (23%)
  waiting for transfers between devices  36.4 us (21%)
  other arithmetic  31 us (18%)
  matrix products  24 us (14%)
  local copies, waits for them, and re-layouts  23.9 us (14%)
  blocking collectives  16.7 us (10%)
    all_to_all x1, blocking collectives, per_device(): lax.all_to_all(coef_local, 'seq', split_axis=0, concat_axis=2, tiled=True)  16.7 us
    all_to_all x1, waiting for transfers between devices, per_device(): lax.all_to_all(gated.T, 'seq', split_axis=0, concat_axis=1, tiled=True)  14.6 us
    unnamed x52, local copies, waits for them, and re-layouts  13 us
    all_to_all x1, starting transfers between devices, per_device(): lax.all_to_all(gated.T, 'seq', split_axis=0, concat_axis=1, tiled=True)  11.4 us
    ppermute x6, starting transfers between devices, taken_together(): value = value + lax.ppermute(value, axis, pairs)  11 us
    dot_general x2, matrix products, local_freq(): jnp.einsum('ckm,mj->ckj', flat, forward_second, preferred_element_type=jn...  8.86 us
    all_to_all x1, waiting for transfers between devices, per_device(): lax.all_to_all(normed.T, 'seq', split_axis=0, concat_axis=1, tiled=True)  8.58 us
    all_to_all x1, starting transfers between devices, per_device(): lax.all_to_all(normed.T, 'seq', split_axis=0, concat_axis=1, tiled=True)  8.5 us
  transfers between devices with their start and end apart: 9, of which 5 were waited for; matrix products, arithmetic and copies ran while one was open for 39% of the time, Pallas kernels for 0%

profile of v2, /device:TPU:1, one launch (start us, length us, event | category | flops | bytes accessed | tf_op | source)
XLA Modules:
  0.0 172.5 jit_solution(8910754822148029757)
XLA Ops:
  0.6 1.5 copy.99
  2.4 3.6 %collective-permute-start = (f32[2048]{0:T(1024)S(1)}, f32[2048]{0:T(1024)S(1)}, u32[]{:S(2)}, u32[]{:S(2)}) collective-permute-start(f32[2048]{0:T(1024)S(1)} %fusion), channel_id=1, source_target_pairs={{0,4},{1,5},{2,6},{3,7},{4,0},{5,1},{6,2},{7,3},{8,12},{9,13},{10,... | collective-permute-start | bytes 24584 | tf_op jit(solution)/shard_map/ppermute | solution.py:26
  8.9 2.3 %copy.98 = bf16[2048,256]{0,1:T(8,128)(2,1)} copy(bf16[2048,256]{1,0:T(8,128)(2,1)} %param.7) | data formatting | bytes 2097152 | tf_op args[1]
  11.2 2.3 %broadcast_select_fusion.2 = bf16[2048,256]{0,1:T(8,128)(2,1)} fusion(bf16[2048,256]{0,1:T(8,128)(2,1)} %copy.98, pred[2048]{0:T(1024)(128)(4,1)S(1)} %fusion.78), kind=kLoop, calls=%fused_computation.57 | loop fusion | flops 524288 | bytes 2099200 | tf_op jit(solution)/shard_map/jit(_where)/select_n | solution.py:100
  13.7 3.1 %broadcast_select_fusion = (bf16[2,512,512]{1,0,2:T(2,128)(2,1)S(1)}, bf16[2,512,512]{1,0,2:T(2,128)(2,1)S(1)}) fusion(pred[2]{0:T(512)(128)(4,1)S(1)} %iota_compare_fusion.1, bf16[512,512]{0,1:T(8,128)(2,1)S(1)} %get-tuple-element.60, f32[512,512]{0,1:T(8,128)S(1)} %bitcast.126, bf16[512,512]{0,1:T(8,128)(2,1)S(1)} %get-tuple-element.61, ...), kind=kLoop, calls=%fused_computation.38 | loop fusion | flops 1048576 | bytes 5242882 | tf_op jit(solution)/shard_map/jit(_where)/select_n | solution.py:51
  16.8 4.6 %select_convert_fusion = (bf16[2,512,2,512]{1,0,3,2:T(2,128)(2,1)S(1)}, bf16[2,512,2,512]{1,0,3,2:T(2,128)(2,1)}) fusion(pred[2,2]{0,1:T(4,128)(4,1)S(1)} %iota_compare_fusion, bf16[2,512,512]{1,0,2:T(2,128)(2,1)S(1)} %get-tuple-element.48, bf16[512,512]{0,1:T(8,128)(2,1)S(1)} %bitcast.140, bf16[2,512,512]{1,0,2:T(2,128)(2,1)S(1)} %get-tuple-element.49), kind=kLoop, calls=%fused_computation | loop fusion | flops 2097152 | bytes 6815748 | tf_op jit(solution)/shard_map/convert_element_type | solution.py:103
  24.2 2.1 %collective-permute-start.2 = (f32[2048]{0:T(1024)S(1)}, f32[2048]{0:T(1024)S(1)}, u32[]{:S(2)}, u32[]{:S(2)}) collective-permute-start(f32[2048]{0:T(1024)S(1)} %add.240), channel_id=1, source_target_pairs={{0,1},{1,0},{2,3},{3,2},{4,5},{5,4},{6,7},{7,6},{8,9},{9,8},{10,11... | collective-permute-start | bytes 24584 | tf_op jit(solution)/shard_map/ppermute | solution.py:26
  27.0 3.5 %copy.139 = bf16[128,8,2,512]{3,1,2,0:T(8,128)(2,1)} copy(bf16[128,8,2,512]{3,2,1,0:T(2,128)(2,1)} %bitcast.131) | data formatting | bytes 4194304
  30.8 2.0 %copy.140 = bf16[128,8,2,512]{3,1,2,0:T(8,128)(2,1)} copy(bf16[128,8,2,512]{3,2,1,0:T(2,128)(2,1)S(1)} %bitcast.130) | data formatting | bytes 4194304
  33.5 11.4 %all-to-all-start = ((bf16[32,8,2048]{2,1,0:T(8,128)(2,1)}), bf16[32,8,2048]{2,1,0:T(8,128)(2,1)S(1)}, u32[]{:S(2)}, u32[]{:S(2)}) async-start(bf16[32,8,2048]{2,1,0:T(8,128)(2,1)} %bitcast.12), calls=%async_computation | async-start | bytes 2097152 | tf_op jit(solution)/shard_map/all_to_all | solution.py:110
  44.9 1.6 fusion.32
  48.4 5.1 %fusion.22 = f32[8,128,2,512]{3,1,2,0:T(8,128)} fusion(f32[8,128,2,64]{3,1,2,0:T(8,128)S(1)} %get-tuple-element.44, f32[8,128,2,64]{3,1,2,0:T(8,128)S(1)} %get-tuple-element.43, f32[512,64]{0,1:T(8,128)S(1)} %get-tuple-element.55, f32[512,64]{0,1:T(8,128)S(1)} %get-tuple-element.54), kind=kOutput, calls=%fused_computation.45 | convolution fusion | flops 1610940416 | bytes 5505024 | tf_op jit(solution)/shard_map/ckrj,bj->ckrb/dot_general | solution.py:134
  55.5 14.6 %all-to-all-done = bf16[32,8,2048]{2,1,0:T(8,128)(2,1)S(1)} async-done(((bf16[32,8,2048]{2,1,0:T(8,128)(2,1)}), bf16[32,8,2048]{2,1,0:T(8,128)(2,1)S(1)}, u32[]{:S(2)}, u32[]{:S(2)}) %all-to-all-start) | async-done | bytes 1048608 | tf_op jit(solution)/shard_map/all_to_all | solution.py:110
  72.0 2.4 %copy.105 = bf16[8,128,2,512]{1,3,2,0:T(8,128)(2,1)} copy(bf16[8,128,2,512]{3,1,0,2:T(8,128)(2,1)S(1)} %pad_maximum_fusion) | data formatting | bytes 4194304 | tf_op jit(solution)/shard_map/stack | solution.py:63
  74.5 8.5 %all-to-all-start.1 = ((bf16[32,8,2048]{2,1,0:T(8,128)(2,1)}), bf16[32,8,2048]{2,1,0:T(8,128)(2,1)}, u32[]{:S(2)}, u32[]{:S(2)}) async-start(bf16[32,8,2048]{2,1,0:T(8,128)(2,1)} %bitcast.132), calls=%async_computation.1 | async-start | bytes 2097152 | tf_op jit(solution)/shard_map/all_to_all | solution.py:112
  83.0 4.1 %fusion.94 = f32[8,128,2,512]{3,1,2,0:T(8,128)S(1)} fusion(bf16[8,128,1024,1]{1,2,3,0:T(8,128)(2,1)} %bitcast.137, bf16[2,512,1024,1]{2,1,0,3:T(8,128)(2,1)S(1)} %bitcast.135), kind=kOutput, calls=%fused_computation.164 | convolution fusion | flops 2147483648 | bytes 8388608 | tf_op jit(solution)/shard_map/ckm,mj->ckj/dot_general | solution.py:123
  89.4 2.4 %copy.107 = bf16[8,128,2,512]{1,3,2,0:T(8,128)(2,1)} copy(bf16[8,128,2,512]{3,1,2,0:T(8,128)(2,1)S(1)} %pad_maximum_fusion.1) | data formatting | bytes 4194304 | tf_op jit(solution)/shard_map/stack | solution.py:140
  91.8 4.6 %fusion.95 = f32[8,128,2,512]{3,1,0,2:T(8,128)S(1)} fusion(bf16[8,128,1024,1]{1,2,0,3:T(8,128)(2,1)} %bitcast.138, bf16[2,512,1024,1]{2,1,3,0:T(8,128)(2,1)} %bitcast.136), kind=kOutput, calls=%fused_computation.165 | convolution fusion | flops 2147483648 | bytes 8388608 | tf_op jit(solution)/shard_map/ckm,mj->ckj/dot_general | solution.py:142
  97.7 1.6 copy.141
  99.2 8.6 %all-to-all-done.1 = bf16[32,8,2048]{2,1,0:T(8,128)(2,1)} async-done(((bf16[32,8,2048]{2,1,0:T(8,128)(2,1)}), bf16[32,8,2048]{2,1,0:T(8,128)(2,1)}, u32[]{:S(2)}, u32[]{:S(2)}) %all-to-all-start.1) | async-done | bytes 1048608 | tf_op jit(solution)/shard_map/all_to_all | solution.py:112
  107.8 8.4 %all-to-all-start.2 = ((bf16[8,32,2048]{2,0,1:T(8,128)(2,1)}), bf16[8,32,2048]{2,0,1:T(8,128)(2,1)S(1)}, u32[]{:S(2)}, u32[]{:S(2)}) async-start(bf16[8,32,2048]{2,0,1:T(8,128)(2,1)} %bitcast.47), calls=%async_computation.2 | async-start | bytes 2097152 | tf_op jit(solution)/shard_map/all_to_all | solution.py:171
  116.2 2.2 %convolution_bitcast_fusion = f32[8,128,2,512]{3,1,0,2:T(8,128)S(1)} fusion(bf16[8,128,512]{2,0,1:T(8,128)(2,1)} %bitcast.39, bf16[128,128,1]{0,1,2:T(8,128)(2,1)S(1)} %bitcast.142, bf16[128,128,1]{0,1,2:T(8,128)(2,1)S(1)} %bitcast.145), kind=kOutput, calls=%fused_computation.6 | convolution fusion | flops 268566528 | bytes 5308416 | tf_op jit(solution)/shard_map/cnm,nkr->ckrm/dot_general | solution.py:118
  119.2 1.6 pad_maximum_fusion.2
  120.7 4.0 %copy.113 = bf16[8,128,2,512]{1,3,2,0:T(8,128)(2,1)} copy(bf16[8,128,2,512]{3,1,0,2:T(8,128)(2,1)} %pad_maximum_fusion.2) | data formatting | bytes 4194304 | tf_op jit(solution)/shard_map/stack | solution.py:63
  124.7 4.7 %fusion.96 = f32[8,128,2,512]{3,1,2,0:T(8,128)S(1)} fusion(bf16[8,128,1024,1]{1,2,3,0:T(8,128)(2,1)} %bitcast.139, bf16[2,512,1024,1]{2,1,0,3:T(8,128)(2,1)} %bitcast.134), kind=kOutput, calls=%fused_computation.166 | convolution fusion | flops 2147483648 | bytes 8388608 | tf_op jit(solution)/shard_map/ckm,mj->ckj/dot_general | solution.py:123
  130.8 1.8 %fusion.10 = f32[8,128,2,128]{3,1,2,0:T(8,128)S(1)} fusion(bf16[8,128,1,512]{3,1,2,0:T(8,128)(2,1)S(1)} %get-tuple-element.27, bf16[8,128,1,512]{3,1,2,0:T(8,128)(2,1)S(1)} %get-tuple-element.26, f32[512,64]{0,1:T(8,128)S(1)} %copy-done.11, f32[512,64]{0,1:T(8,128)S(1)} %copy-done.9), kind=kOutput, calls=%fused_computation.22 | convolution fusion | flops 1611726848 | bytes 3407872 | tf_op jit(solution)/shard_map/ckrb,bj->ckrj/dot_general | solution.py:162
  133.0 8.1 %all-to-all-done.2 = bf16[8,32,2048]{2,0,1:T(8,128)(2,1)S(1)} async-done(((bf16[8,32,2048]{2,0,1:T(8,128)(2,1)}), bf16[8,32,2048]{2,0,1:T(8,128)(2,1)S(1)}, u32[]{:S(2)}, u32[]{:S(2)}) %all-to-all-start.2) | async-done | bytes 1048608 | tf_op jit(solution)/shard_map/all_to_all | solution.py:171
  141.1 1.8 %fusion.3 = f32[2048]{0:T(1024)S(1)} fusion(bf16[2048,256]{0,1:T(8,128)(2,1)S(1)} %copy.99, bf16[2048,256]{0,1:T(8,128)(2,1)} %broadcast_select_fusion.2, bf16[256,2048]{1,0:T(8,128)(2,1)S(1)} %bitcast.128, f32[256]{0:T(256)S(1)} %copy-done.18, f32[256]{0:T(256)S(1)} %copy-done.17), kind=kLoop, calls=%fused_computation.11 | loop fusion | flops 4192256 | bytes 3155968 | tf_op jit(solution)/shard_map/reduce_sum | solution.py:178
  143.4 3.7 %collective-permute-done.3 = f32[2048]{0:T(1024)S(1)} collective-permute-done((f32[2048]{0:T(1024)S(1)}, f32[2048]{0:T(1024)S(1)}, u32[]{:S(2)}, u32[]{:S(2)}) %collective-permute-start.3) | collective-permute-done | bytes 8224 | tf_op jit(solution)/shard_map/ppermute | solution.py:26
  147.5 16.7 %all_to_all.66 = f32[64,2,8]{2,1,0:T(2,128)S(1)} all-to-all(f32[64,2,8]{2,1,0:T(2,128)S(1)} %copy.118), channel_id=1, replica_groups=mesh['seq'=32,'ch'=8] {'seq'}, dimensions={0} | all-to-all | bytes 8192 | tf_op jit(solution)/shard_map/all_to_all | solution.py:173
  164.3 4.1 %collective-permute-start.5 = (f32[2048]{0:T(1024)S(1)}, f32[2048]{0:T(1024)S(1)}, u32[]{:S(2)}, u32[]{:S(2)}) collective-permute-start(f32[2048]{0:T(1024)S(1)} %add.262), channel_id=1, source_target_pairs={{0,1},{1,0},{2,3},{3,2},{4,5},{5,4},{6,7},{7,6},{8,9},{9,8},{10,11... | collective-permute-start | bytes 24584 | tf_op jit(solution)/shard_map/ppermute | solution.py:26
  169.2 1.9 %fusion.5 = bf16[2048,256]{0,1:T(8,128)(2,1)S(1)} fusion(bf16[2048,256]{0,1:T(8,128)(2,1)S(1)} %copy.99, bf16[2048,256]{0,1:T(8,128)(2,1)} %broadcast_select_fusion.2, bf16[256,2048]{1,0:T(8,128)(2,1)S(1)} %bitcast.129, f32[2048]{0:T(1024)S(1)} %fusion.80, f32[256]{0:T(256)S(1)} %copy-done.18, f32[256]{0:T(256)S(1)} %copy-done.17, f32[2048]{0:T(1024)S(1)} %add_rsqrt_fusion), kind=kLoop, calls=%fused_computation.13 | loop fusion | flops 5242880 | bytes 4212736 | tf_op jit(solution)/shard_map/convert_element_type | solution.py:182
  (109 shorter events, 22.3 us)
Async XLA Ops:
  2.1 6.3 %copy-start.21 = (s32[64]{0:T(128)S(1)}, s32[64]{0:T(128)}, u32[]{:S(2)}) copy-start(s32[64]{0:T(128)} %param.11) | copy-start | bytes 772
  2.4 19.2 %collective-permute-start = (f32[2048]{0:T(1024)S(1)}, f32[2048]{0:T(1024)S(1)}, u32[]{:S(2)}, u32[]{:S(2)}) collective-permute-start(f32[2048]{0:T(1024)S(1)} %fusion), channel_id=1, source_target_pairs={{0,4},{1,5},{2,6},{3,7},{4,0},{5,1},{6,2},{7,3},{8,12},{9,13},{10,... | collective-permute-start | bytes 24584 | tf_op jit(solution)/shard_map/ppermute | solution.py:26
  8.4 12.9 %copy-start.19 = (s32[64]{0:T(128)}, s32[64]{0:T(128)S(1)}, u32[]{:S(2)}) copy-start(s32[64]{0:T(128)S(1)} %multiply_add_fusion.2) | copy-start | bytes 772
  13.7 3.1 %copy-start.6 = (bf16[512,8,64]{0,2,1:T(8,128)(2,1)S(1)}, bf16[512,8,64]{0,2,1:T(8,128)(2,1)}, u32[]{:S(2)}) copy-start(bf16[512,8,64]{0,2,1:T(8,128)(2,1)} %subtract_multiply_fusion) | copy-start | bytes 1572868
  16.7 9.6 %copy-start.16 = (bf16[64,2,256]{2,1,0:T(2,128)(2,1)S(1)}, bf16[64,2,256]{2,1,0:T(2,128)(2,1)}, u32[]{:S(2)}) copy-start(bf16[64,2,256]{2,1,0:T(2,128)(2,1)} %param.10) | copy-start | bytes 196612
  16.8 9.7 %copy-start.22 = (bf16[256]{0:T(256)(128)(2,1)S(1)}, bf16[256]{0:T(256)(128)(2,1)}, u32[]{:S(2)}) copy-start(bf16[256]{0:T(256)(128)(2,1)} %param.8) | copy-start | bytes 1540
  21.6 2.6 %collective-permute-start.1 = (f32[2048]{0:T(1024)S(1)}, f32[2048]{0:T(1024)S(1)}, u32[]{:S(2)}, u32[]{:S(2)}) collective-permute-start(f32[2048]{0:T(1024)S(1)} %add.239), channel_id=1, source_target_pairs={{0,2},{1,3},{2,0},{3,1},{4,6},{5,7},{6,4},{7,5},{8,10},{9,11},{10,... | collective-permute-start | bytes 24584 | tf_op jit(solution)/shard_map/ppermute | solution.py:26
  24.2 9.3 %collective-permute-start.2 = (f32[2048]{0:T(1024)S(1)}, f32[2048]{0:T(1024)S(1)}, u32[]{:S(2)}, u32[]{:S(2)}) collective-permute-start(f32[2048]{0:T(1024)S(1)} %add.240), channel_id=1, source_target_pairs={{0,1},{1,0},{2,3},{3,2},{4,5},{5,4},{6,7},{7,6},{8,9},{9,8},{10,11... | collective-permute-start | bytes 24584 | tf_op jit(solution)/shard_map/ppermute | solution.py:26
  32.8 14.7 %copy-start.20 = (s32[64]{0:T(128)S(1)}, s32[64]{0:T(128)}, u32[]{:S(2)}) copy-start(s32[64]{0:T(128)} %copy-done.19) | copy-start | bytes 772
  33.5 36.6 %all-to-all-start = ((bf16[32,8,2048]{2,1,0:T(8,128)(2,1)}), bf16[32,8,2048]{2,1,0:T(8,128)(2,1)S(1)}, u32[]{:S(2)}, u32[]{:S(2)}) async-start(bf16[32,8,2048]{2,1,0:T(8,128)(2,1)} %bitcast.12), calls=%async_computation | async-start | bytes 2097152 | tf_op jit(solution)/shard_map/all_to_all | solution.py:110
  47.5 23.6 %copy-start.3 = (f32[128,512]{1,0:T(8,128)}, f32[128,512]{1,0:T(8,128)S(1)}, u32[]{:S(2)}) copy-start(f32[128,512]{1,0:T(8,128)S(1)} %get-tuple-element.59) | copy-start | bytes 786436
  48.1 5.4 %copy-start.8 = (f32[512,64]{0,1:T(8,128)}, f32[512,64]{0,1:T(8,128)S(1)}, u32[]{:S(2)}) copy-start(f32[512,64]{0,1:T(8,128)S(1)} %get-tuple-element.54) | copy-start | bytes 393220
  48.1 5.4 %copy-start.10 = (f32[512,64]{0,1:T(8,128)}, f32[512,64]{0,1:T(8,128)S(1)}, u32[]{:S(2)}) copy-start(f32[512,64]{0,1:T(8,128)S(1)} %get-tuple-element.55) | copy-start | bytes 393220
  48.3 5.3 %copy-start.13 = (f32[128,64]{0,1:T(8,128)S(1)}, f32[128,64]{0,1:T(8,128)}, u32[]{:S(2)}) copy-start(f32[128,64]{0,1:T(8,128)} %get-tuple-element.56) | copy-start | bytes 98308
  48.4 5.3 %copy-start.14 = (f32[128,64]{0,1:T(8,128)S(1)}, f32[128,64]{0,1:T(8,128)}, u32[]{:S(2)}) copy-start(f32[128,64]{0,1:T(8,128)} %get-tuple-element.57) | copy-start | bytes 98308
  48.4 5.9 %copy-start.17 = (f32[256]{0:T(256)S(1)}, f32[256]{0:T(256)}, u32[]{:S(2)}) copy-start(f32[256]{0:T(256)} %convert_element_type.207) | copy-start | bytes 3076
  74.5 8.5 %copy-start.5 = (bf16[128,8,2,512]{3,1,2,0:T(8,128)(2,1)S(1)}, bf16[128,8,2,512]{3,1,2,0:T(8,128)(2,1)}, u32[]{:S(2)}) copy-start(bf16[128,8,2,512]{3,1,2,0:T(8,128)(2,1)} %copy.139) | copy-start | bytes 6291460
  74.5 33.3 %all-to-all-start.1 = ((bf16[32,8,2048]{2,1,0:T(8,128)(2,1)}), bf16[32,8,2048]{2,1,0:T(8,128)(2,1)}, u32[]{:S(2)}, u32[]{:S(2)}) async-start(bf16[32,8,2048]{2,1,0:T(8,128)(2,1)} %bitcast.132), calls=%async_computation.1 | async-start | bytes 2097152 | tf_op jit(solution)/shard_map/all_to_all | solution.py:112
  83.0 4.1 %copy-start.2 = (f32[8,128,2,512]{3,1,2,0:T(8,128)S(1)}, f32[8,128,2,512]{3,1,2,0:T(8,128)}, u32[]{:S(2)}) copy-start(f32[8,128,2,512]{3,1,2,0:T(8,128)} %fusion.22) | copy-start | bytes 12582916
  87.1 2.0 %copy-start = (f32[8,128,2,512]{3,1,2,0:T(8,128)}, f32[8,128,2,512]{3,1,2,0:T(8,128)S(1)}, u32[]{:S(2)}) copy-start(f32[8,128,2,512]{3,1,2,0:T(8,128)S(1)} %fusion.94) | copy-start | bytes 12582916
  91.8 4.6 %copy-start.7 = (f32[128,512]{1,0:T(8,128)S(1)}, f32[128,512]{1,0:T(8,128)}, u32[]{:S(2)}) copy-start(f32[128,512]{1,0:T(8,128)} %fusion.32) | copy-start | bytes 786436
  96.5 0.8 copy-start.15
  107.8 33.3 %all-to-all-start.2 = ((bf16[8,32,2048]{2,0,1:T(8,128)(2,1)}), bf16[8,32,2048]{2,0,1:T(8,128)(2,1)S(1)}, u32[]{:S(2)}, u32[]{:S(2)}) async-start(bf16[8,32,2048]{2,0,1:T(8,128)(2,1)} %bitcast.47), calls=%async_computation.2 | async-start | bytes 2097152 | tf_op jit(solution)/shard_map/all_to_all | solution.py:171
  116.2 2.2 %copy-start.4 = (f32[128,512]{1,0:T(8,128)S(1)}, f32[128,512]{1,0:T(8,128)}, u32[]{:S(2)}) copy-start(f32[128,512]{1,0:T(8,128)} %copy-done.3) | copy-start | bytes 786436
  124.7 4.8 %copy-start.1 = (f32[8,128,2,512]{3,1,2,0:T(8,128)S(1)}, f32[8,128,2,512]{3,1,2,0:T(8,128)}, u32[]{:S(2)}) copy-start(f32[8,128,2,512]{3,1,2,0:T(8,128)} %copy-done) | copy-start | bytes 12582916
  129.5 1.3 copy-start.9
  129.5 1.3 copy-start.11
  130.7 1.9 %copy-start.12 = (f32[128,64]{1,0:T(8,128)S(1)}, f32[128,64]{1,0:T(8,128)}, u32[]{:S(2)}) copy-start(f32[128,64]{1,0:T(8,128)} %copy.117) | copy-start | bytes 98308
  132.6 8.5 %copy-start.18 = (f32[256]{0:T(256)S(1)}, f32[256]{0:T(256)}, u32[]{:S(2)}) copy-start(f32[256]{0:T(256)} %param.9) | copy-start | bytes 3076
  143.0 4.1 %collective-permute-start.3 = (f32[2048]{0:T(1024)S(1)}, f32[2048]{0:T(1024)S(1)}, u32[]{:S(2)}, u32[]{:S(2)}) collective-permute-start(f32[2048]{0:T(1024)S(1)} %fusion.3), channel_id=1, source_target_pairs={{0,4},{1,5},{2,6},{3,7},{4,0},{5,1},{6,2},{7,3},{8,12},{9,13},{10,... | collective-permute-start | bytes 24584 | tf_op jit(solution)/shard_map/ppermute | solution.py:26
  147.1 17.2 %collective-permute-start.4 = (f32[2048]{0:T(1024)S(1)}, f32[2048]{0:T(1024)S(1)}, u32[]{:S(2)}, u32[]{:S(2)}) collective-permute-start(f32[2048]{0:T(1024)S(1)} %add.261), channel_id=1, source_target_pairs={{0,2},{1,3},{2,0},{3,1},{4,6},{5,7},{6,4},{7,5},{8,10},{9,11},{10,... | collective-permute-start | bytes 24584 | tf_op jit(solution)/shard_map/ppermute | solution.py:26
  164.3 4.9 %collective-permute-start.5 = (f32[2048]{0:T(1024)S(1)}, f32[2048]{0:T(1024)S(1)}, u32[]{:S(2)}, u32[]{:S(2)}) collective-permute-start(f32[2048]{0:T(1024)S(1)} %add.262), channel_id=1, source_target_pairs={{0,1},{1,0},{2,3},{3,2},{4,5},{5,4},{6,7},{7,6},{8,9},{9,8},{10,11... | collective-permute-start | bytes 24584 | tf_op jit(solution)/shard_map/ppermute | solution.py:26

commit v3 on v0

--- a/solution.py
+++ b/solution.py
@@ -49,8 +49,7 @@
     same = (half[:, None, None, None] == half[None, None, :, None])
     upper = half[:, None, None, None] == 0
     sine_signed = jnp.where(upper, sine_part[None, :, None, :], -sine_part[None, :, None, :])
-    whole = jnp.where(same, cosine[None, :, None, :], sine_signed)
-    return whole.reshape(2 * count, 2 * count)
+    return jnp.where(same, cosine[None, :, None, :], sine_signed)
 
 
 def twist_leading(parts, freq_index, pos_index, seq_total, sign):
@@ -119,11 +118,9 @@
             "cnm,nkr->ckrm", blocks, forward_first, preferred_element_type=jnp.float32
         )
         turned = twist_leading(parts, block_ids, all_inner, seq_total, -1.0).astype(jnp.bfloat16)
-        flat = turned.reshape(width_share, nblocks, 2 * BLOCK)
-        spectrum = jnp.einsum(
-            "ckm,mj->ckj", flat, forward_second, preferred_element_type=jnp.float32
+        return jnp.einsum(
+            "ckrm,rmsj->cksj", turned, forward_second, preferred_element_type=jnp.float32
         )
-        return spectrum.reshape(width_share, nblocks, 2, BLOCK)
 
     spec_gated = local_freq(moved[1])
     inner_tab, block_cos, block_sin = feature_factors(BLOCK, nblocks, seq_total)
@@ -138,11 +135,9 @@
     prod_real = response[:, :, 0] * spec_gated[:, :, 0] + response[:, :, 1] * spec_gated[:, :, 1]
     prod_imag = response[:, :, 0] * spec_gated[:, :, 1] - response[:, :, 1] * spec_gated[:, :, 0]
     product = jnp.stack([prod_real, prod_imag], axis=2).astype(jnp.bfloat16)
-    flat_product = product.reshape(width_share, nblocks, 2 * BLOCK)
     back_parts = jnp.einsum(
-        "ckm,mj->ckj", flat_product, back_first, preferred_element_type=jnp.float32
+        "ckrm,rmsj->cksj", product, back_first, preferred_element_type=jnp.float32
     )
-    back_parts = back_parts.reshape(width_share, nblocks, 2, BLOCK)
     back_twisted = twist_leading(back_parts, block_ids, all_inner, seq_total, 1.0).astype(
         jnp.bfloat16
     )

time: 170 us -> 156 us (0.918)
  matrix products: 24 us -> 17.9 us
  local copies, waits for them, and re-layouts: 23.9 us -> 19.1 us
  waiting for transfers between devices: 35 us -> 31 us
  starting transfers between devices: 39.4 us -> 42.8 us
  other arithmetic: 31 us -> 27.7 us
    another operation x4 -> x1, local copies, waits for them, and re-layouts: 8.94 us -> 0.1 us  [the longest x2 6.41 us: twist_leading(): return jnp.stack([real_part, imag_part], axis=2)]
    all_to_all x1, waiting for transfers between devices: 14.2 us -> 6.13 us  [per_device(): lax.all_to_all(gated.T, 'seq', split_axis=0, concat_axis=1, tiled=True)]
    dot_general x3, matrix products: 13.5 us -> 7.44 us  [the longest x2 4.93 us: local_freq(): jnp.einsum('ckrm,rmsj->cksj', turned, forward_second, preferred_element_t...]
    ppermute x6, starting transfers between devices: 11.2 us -> 16.6 us  [taken_together(): value = value + lax.ppermute(value, axis, pairs)]
    convert_element_type x1 -> x0, other arithmetic: 4.58 us -> none  [per_device(): back_first = block_matrix(BLOCK, 1.0).astype(jnp.bfloat16)]
    neg x0 -> x2, local copies, waits for them, and re-layouts: none -> 4.14 us  [block_matrix(): -sine_part[None, :, None, :]]
    unnamed x52 -> x60, local copies, waits for them, and re-layouts: 13 us -> 8.88 us
    mul x0 -> x3, local copies, waits for them, and re-layouts: none -> 3.28 us  [twin_table(): return (cosine * factor, sign * sine * factor)]
  transfers between devices with their start and end apart: 9 -> 9, of which waited for: 6 -> 7; matrix products, arithmetic and copies ran while one was open for 40% -> 36% of each run, Pallas kernels for 0% -> 0%
where the time goes in v3:
time: 156 us; the launch traced here: 153 us
  starting transfers between devices  42.8 us (27%)
  waiting for transfers between devices  31 us (20%)
  other arithmetic  27.7 us (18%)
  local copies, waits for them, and re-layouts  19.1 us (12%)
  matrix products  17.9 us (11%)
  blocking collectives  13.4 us (9%)
    ppermute x6, starting transfers between devices, taken_together(): value = value + lax.ppermute(value, axis, pairs)  16.6 us
    all_to_all x1, blocking collectives, per_device(): lax.all_to_all(coef_local, 'seq', split_axis=0, concat_axis=2, tiled=True)  13.4 us
    all_to_all x1, waiting for transfers between devices, per_device(): lax.all_to_all(time_field, 'seq', split_axis=1, concat_axis=0, tiled=True)  11.2 us
    all_to_all x1, starting transfers between devices, per_device(): lax.all_to_all(gated.T, 'seq', split_axis=0, concat_axis=1, tiled=True)  9.63 us
    all_to_all x1, starting transfers between devices, per_device(): lax.all_to_all(time_field, 'seq', split_axis=1, concat_axis=0, tiled=True)  9.34 us
    unnamed x60, local copies, waits for them, and re-layouts  8.88 us
    all_to_all x1, waiting for transfers between devices, per_device(): lax.all_to_all(normed.T, 'seq', split_axis=0, concat_axis=1, tiled=True)  7.8 us
    all_to_all x1, starting transfers between devices, per_device(): lax.all_to_all(normed.T, 'seq', split_axis=0, concat_axis=1, tiled=True)  7.2 us
  transfers between devices with their start and end apart: 9, of which 7 were waited for; matrix products, arithmetic and copies ran while one was open for 36% of the time, Pallas kernels for 0%

profile of v3, /device:TPU:1, one launch (start us, length us, event | category | flops | bytes accessed | tf_op | source)
XLA Modules:
  0.0 153.1 jit_solution(16032689114085163433)
XLA Ops:
  0.6 1.5 copy.102
  2.4 3.3 %collective-permute-start = (f32[2048]{0:T(1024)S(1)}, f32[2048]{0:T(1024)S(1)}, u32[]{:S(2)}, u32[]{:S(2)}) collective-permute-start(f32[2048]{0:T(1024)S(1)} %fusion), channel_id=1, source_target_pairs={{0,1},{1,0},{2,3},{3,2},{4,5},{5,4},{6,7},{7,6},{8,9},{9,8},{10,11... | collective-permute-start | bytes 24584 | tf_op jit(solution)/shard_map/ppermute | solution.py:26
  6.4 1.6 %fusion.51 = (f32[128,512]{1,0:T(8,128)S(1)}, f32[128,512]{1,0:T(8,128)}) fusion(), kind=kLoop, calls=%fused_computation.82 | loop fusion | flops 262144 | bytes 524288 | tf_op jit(solution)/shard_map/cos | solution.py:58
  11.0 1.6 %fusion.50 = f32[128,512]{1,0:T(8,128)} fusion(), kind=kLoop, calls=%fused_computation.81 | loop fusion | flops 196608 | bytes 262144 | tf_op jit(solution)/shard_map/sin | solution.py:59
  13.0 2.3 %copy.101 = bf16[2048,256]{0,1:T(8,128)(2,1)} copy(bf16[2048,256]{1,0:T(8,128)(2,1)} %param.7) | data formatting | bytes 2097152 | tf_op args[1]
  16.1 2.3 %broadcast_select_fusion.2 = bf16[2048,256]{0,1:T(8,128)(2,1)} fusion(bf16[2048,256]{0,1:T(8,128)(2,1)} %copy.101, pred[2048]{0:T(1024)(128)(4,1)S(1)} %fusion.96), kind=kLoop, calls=%fused_computation.75 | loop fusion | flops 524288 | bytes 2099200 | tf_op jit(solution)/shard_map/jit(_where)/select_n | solution.py:99
  21.1 1.9 %collective-permute-done.1 = f32[2048]{0:T(1024)S(1)} collective-permute-done((f32[2048]{0:T(1024)S(1)}, f32[2048]{0:T(1024)S(1)}, u32[]{:S(2)}, u32[]{:S(2)}) %collective-permute-start.1) | collective-permute-done | bytes 8224 | tf_op jit(solution)/shard_map/ppermute | solution.py:26
  24.6 2.4 %collective-permute-done.2 = f32[2048]{0:T(1024)S(1)} collective-permute-done((f32[2048]{0:T(1024)S(1)}, f32[2048]{0:T(1024)S(1)}, u32[]{:S(2)}, u32[]{:S(2)}) %collective-permute-start.2) | collective-permute-done | bytes 8224 | tf_op jit(solution)/shard_map/ppermute | solution.py:26
  27.0 9.6 %all-to-all-start = ((bf16[32,8,2048]{2,1,0:T(8,128)(2,1)}), bf16[32,8,2048]{2,1,0:T(8,128)(2,1)}, u32[]{:S(2)}, u32[]{:S(2)}) async-start(bf16[32,8,2048]{2,1,0:T(8,128)(2,1)} %bitcast.12), calls=%async_computation | async-start | bytes 2097152 | tf_op jit(solution)/shard_map/all_to_all | solution.py:109
  37.8 2.1 %copy.110 = bf16[512,512]{1,0:T(8,128)(2,1)} copy(bf16[512,512]{0,1:T(8,128)(2,1)} %get-tuple-element.59) | data formatting | bytes 1048576 | tf_op jit(solution)/shard_map/neg | solution.py:51
  39.9 2.1 %copy.113 = bf16[512,512]{1,0:T(8,128)(2,1)} copy(bf16[512,512]{0,1:T(8,128)(2,1)} %get-tuple-element.58) | data formatting | bytes 1048576 | tf_op jit(solution)/shard_map/neg | solution.py:51
  43.2 2.1 %copy.108 = bf16[512,512]{1,0:T(8,128)(2,1)} copy(bf16[512,512]{0,1:T(8,128)(2,1)} %bitcast.118) | data formatting | bytes 1048576 | tf_op jit(solution)/shard_map/mul | solution.py:43
  46.5 5.1 %fusion.40 = f32[8,128,2,512]{3,1,2,0:T(8,128)} fusion(f32[8,128,2,64]{3,1,2,0:T(8,128)S(1)} %get-tuple-element.42, f32[8,128,2,64]{3,1,2,0:T(8,128)S(1)} %get-tuple-element.41, f32[512,64]{0,1:T(8,128)S(1)} %get-tuple-element.53, f32[512,64]{0,1:T(8,128)S(1)} %get-tuple-element.52), kind=kOutput, calls=%fused_computation.61 | convolution fusion | flops 1610940416 | bytes 5505024 | tf_op jit(solution)/shard_map/ckrj,bj->ckrb/dot_general | solution.py:131
  51.8 1.7 %broadcast_select_fusion = (bf16[2,512,512]{2,1,0:T(8,128)(2,1)}, bf16[2,512,512]{2,1,0:T(8,128)(2,1)}) fusion(bf16[512,512]{1,0:T(8,128)(2,1)S(1)} %copy-done.7, bf16[512,512]{1,0:T(8,128)(2,1)S(1)} %copy.112, pred[2]{0:T(512)(128)(4,1)S(1)} %copy-done.25, bf16[512,512]{1,0:T(8,128)(2,1)S(1)} %copy-done.6, bf16[512,512]{1,0:T(8,128)(2,1)S(1)} %copy-done.5), kind=kLoop, calls=%fused_computation.69 | loop fusion | flops 1048576 | bytes 4194306 | tf_op jit(solution)/shard_map/jit(_where)/select_n | solution.py:51
  54.7 6.1 %all-to-all-done = bf16[32,8,2048]{2,1,0:T(8,128)(2,1)} async-done(((bf16[32,8,2048]{2,1,0:T(8,128)(2,1)}), bf16[32,8,2048]{2,1,0:T(8,128)(2,1)}, u32[]{:S(2)}, u32[]{:S(2)}) %all-to-all-start) | async-done | bytes 1048608 | tf_op jit(solution)/shard_map/all_to_all | solution.py:109
  60.9 7.2 %all-to-all-start.1 = ((bf16[32,8,2048]{2,1,0:T(8,128)(2,1)}), bf16[32,8,2048]{2,1,0:T(8,128)(2,1)S(1)}, u32[]{:S(2)}, u32[]{:S(2)}) async-start(bf16[32,8,2048]{2,1,0:T(8,128)(2,1)} %bitcast.35), calls=%async_computation.1 | async-start | bytes 2097152 | tf_op jit(solution)/shard_map/all_to_all | solution.py:111
  68.1 2.2 %convolution_bitcast_fusion.4 = f32[8,128,2,512]{3,1,0,2:T(8,128)S(1)} fusion(bf16[8,128,512]{2,0,1:T(8,128)(2,1)} %bitcast.15, bf16[128,128,1]{0,1,2:T(8,128)(2,1)S(1)} %bitcast.119, bf16[128,128,1]{0,1,2:T(8,128)(2,1)S(1)} %bitcast.121), kind=kOutput, calls=%fused_computation.10 | convolution fusion | flops 268566528 | bytes 5308416 | tf_op jit(solution)/shard_map/cnm,nkr->ckrm/dot_general | solution.py:117
  71.6 2.5 %convolution_bitcast_fusion.3 = f32[8,128,2,512]{3,1,2,0:T(8,128)S(1)} fusion(bf16[2,512,512]{2,1,0:T(8,128)(2,1)S(1)} %copy-done.8, bf16[512,512]{1,0:T(8,128)(2,1)S(1)} %copy-done.16, pred[2,2]{0,1:T(4,128)(4,1)S(1)} %copy-done.27, bf16[8,128,1,512]{3,1,0,2:T(8,128)(2,1)S(1)} %get-tuple-element.35, bf16[8,128,1,512]{3,1,0,2:T(8,128)(2,1)S(1)} %get-tuple-element.34), kind=kOutput, calls=%fused_computation.9 | convolution fusion | flops 2149580800 | bytes 7864324 | tf_op jit(solution)/shard_map/ckrm,rmsj->cksj/dot_general | solution.py:121
  76.4 2.5 %convolution_bitcast_fusion.2 = f32[8,128,2,512]{3,1,0,2:T(8,128)S(1)} fusion(bf16[8,128,1,512]{3,1,2,0:T(8,128)(2,1)S(1)} %get-tuple-element.29, bf16[8,128,1,512]{3,1,2,0:T(8,128)(2,1)S(1)} %get-tuple-element.28, bf16[2,512,512]{2,1,0:T(8,128)(2,1)S(1)} %copy-done.10, bf16[512,512]{1,0:T(8,128)(2,1)S(1)} %copy-done.16, pred[2,2]{0,1:T(4,128)(4,1)S(1)} %copy-done.27), kind=kOutput, calls=%fused_computation.8 | convolution fusion | flops 2152726528 | bytes 7864324 | tf_op jit(solution)/shard_map/ckrm,rmsj->cksj/dot_general | solution.py:138
  80.1 1.6 %copy.145 = bf16[1,8,128,512]{3,1,2,0:T(8,128)(2,1)} copy(bf16[1,8,128,512]{3,2,1,0:T(8,128)(2,1)S(1)} %fusion.35) | data formatting | bytes 2097152
  81.7 7.8 %all-to-all-done.1 = bf16[32,8,2048]{2,1,0:T(8,128)(2,1)S(1)} async-done(((bf16[32,8,2048]{2,1,0:T(8,128)(2,1)}), bf16[32,8,2048]{2,1,0:T(8,128)(2,1)S(1)}, u32[]{:S(2)}, u32[]{:S(2)}) %all-to-all-start.1) | async-done | bytes 1048608 | tf_op jit(solution)/shard_map/all_to_all | solution.py:111
  89.5 9.3 %all-to-all-start.2 = ((bf16[8,32,2048]{2,0,1:T(8,128)(2,1)}), bf16[8,32,2048]{2,0,1:T(8,128)(2,1)S(1)}, u32[]{:S(2)}, u32[]{:S(2)}) async-start(bf16[8,32,2048]{2,0,1:T(8,128)(2,1)} %bitcast.47), calls=%async_computation.2 | async-start | bytes 2097152 | tf_op jit(solution)/shard_map/all_to_all | solution.py:166
  98.8 1.5 copy.121
  102.6 2.5 %convolution_bitcast_fusion = f32[8,128,2,512]{3,1,2,0:T(8,128)S(1)} fusion(bf16[2,512,512]{2,1,0:T(8,128)(2,1)S(1)} %copy-done.9, bf16[512,512]{1,0:T(8,128)(2,1)S(1)} %copy-done.17, pred[2,2]{0,1:T(4,128)(4,1)S(1)} %copy-done.27, bf16[8,128,1,512]{3,1,0,2:T(8,128)(2,1)S(1)} %get-tuple-element.31, bf16[8,128,1,512]{3,1,0,2:T(8,128)(2,1)S(1)} %get-tuple-element.30), kind=kOutput, calls=%fused_computation.6 | convolution fusion | flops 2149580800 | bytes 7864324 | tf_op jit(solution)/shard_map/ckrm,rmsj->cksj/dot_general | solution.py:121
  106.4 1.8 %fusion.17 = f32[8,128,2,128]{3,1,2,0:T(8,128)S(1)} fusion(bf16[8,128,1,512]{3,1,2,0:T(8,128)(2,1)S(1)} %get-tuple-element.27, bf16[8,128,1,512]{3,1,2,0:T(8,128)(2,1)S(1)} %get-tuple-element.26, f32[512,64]{0,1:T(8,128)S(1)} %copy-done.15, f32[512,64]{0,1:T(8,128)S(1)} %copy-done.13), kind=kOutput, calls=%fused_computation.29 | convolution fusion | flops 1611726848 | bytes 3407872 | tf_op jit(solution)/shard_map/ckrb,bj->ckrj/dot_general | solution.py:157
  108.7 11.2 %all-to-all-done.2 = bf16[8,32,2048]{2,0,1:T(8,128)(2,1)S(1)} async-done(((bf16[8,32,2048]{2,0,1:T(8,128)(2,1)}), bf16[8,32,2048]{2,0,1:T(8,128)(2,1)S(1)}, u32[]{:S(2)}, u32[]{:S(2)}) %all-to-all-start.2) | async-done | bytes 1048608 | tf_op jit(solution)/shard_map/all_to_all | solution.py:166
  119.8 1.8 %fusion.3 = f32[2048]{0:T(1024)S(1)} fusion(bf16[2048,256]{0,1:T(8,128)(2,1)S(1)} %copy.102, bf16[2048,256]{0,1:T(8,128)(2,1)} %broadcast_select_fusion.2, bf16[256,2048]{1,0:T(8,128)(2,1)S(1)} %bitcast.115, f32[256]{0:T(256)S(1)} %copy-done.21, f32[256]{0:T(256)S(1)} %convert_element_type.177), kind=kLoop, calls=%fused_computation.14 | loop fusion | flops 4192256 | bytes 3155968 | tf_op jit(solution)/shard_map/reduce_sum | solution.py:173
  121.7 8.5 %collective-permute-start.3 = (f32[2048]{0:T(1024)S(1)}, f32[2048]{0:T(1024)S(1)}, u32[]{:S(2)}, u32[]{:S(2)}) collective-permute-start(f32[2048]{0:T(1024)S(1)} %fusion.3), channel_id=1, source_target_pairs={{0,1},{1,0},{2,3},{3,2},{4,5},{5,4},{6,7},{7,6},{8,9},{9,8},{10,11... | collective-permute-start | bytes 24584 | tf_op jit(solution)/shard_map/ppermute | solution.py:26
  132.3 13.4 %all_to_all.66 = f32[64,2,8]{2,1,0:T(2,128)S(1)} all-to-all(f32[64,2,8]{2,1,0:T(2,128)S(1)} %copy.122), channel_id=1, replica_groups=mesh['seq'=32,'ch'=8] {'seq'}, dimensions={0} | all-to-all | bytes 8192 | tf_op jit(solution)/shard_map/all_to_all | solution.py:168
  145.8 2.5 %collective-permute-start.5 = (f32[2048]{0:T(1024)S(1)}, f32[2048]{0:T(1024)S(1)}, u32[]{:S(2)}, u32[]{:S(2)}) collective-permute-start(f32[2048]{0:T(1024)S(1)} %add.268), channel_id=1, source_target_pairs={{0,4},{1,5},{2,6},{3,7},{4,0},{5,1},{6,2},{7,3},{8,12},{9,13},{10,... | collective-permute-start | bytes 24584 | tf_op jit(solution)/shard_map/ppermute | solution.py:26
  149.9 1.9 %fusion.5 = bf16[2048,256]{0,1:T(8,128)(2,1)S(1)} fusion(bf16[2048,256]{0,1:T(8,128)(2,1)S(1)} %copy.102, bf16[2048,256]{0,1:T(8,128)(2,1)} %broadcast_select_fusion.2, bf16[256,2048]{1,0:T(8,128)(2,1)S(1)} %bitcast.116, f32[2048]{0:T(1024)S(1)} %fusion.98, f32[256]{0:T(256)S(1)} %copy-done.21, f32[256]{0:T(256)S(1)} %convert_element_type.177, ...), kind=kLoop, calls=%fused_computation.16 | loop fusion | flops 5242880 | bytes 4212736 | tf_op jit(solution)/shard_map/convert_element_type | solution.py:177
  151.8 1.3 copy.126
  (115 shorter events, 26.8 us)
Async XLA Ops:
  2.4 18.0 %collective-permute-start = (f32[2048]{0:T(1024)S(1)}, f32[2048]{0:T(1024)S(1)}, u32[]{:S(2)}, u32[]{:S(2)}) collective-permute-start(f32[2048]{0:T(1024)S(1)} %fusion), channel_id=1, source_target_pairs={{0,1},{1,0},{2,3},{3,2},{4,5},{5,4},{6,7},{7,6},{8,9},{9,8},{10,11... | collective-permute-start | bytes 24584 | tf_op jit(solution)/shard_map/ppermute | solution.py:26
  6.4 6.1 %copy-start.24 = (s32[64]{0:T(128)S(1)}, s32[64]{0:T(128)}, u32[]{:S(2)}) copy-start(s32[64]{0:T(128)} %param.11) | copy-start | bytes 772
  12.7 2.6 %copy-start.22 = (s32[64]{0:T(128)S(1)}, s32[64]{0:T(128)}, u32[]{:S(2)}) copy-start(s32[64]{0:T(128)} %multiply_add_fusion.2) | copy-start | bytes 772
  20.4 2.6 %collective-permute-start.1 = (f32[2048]{0:T(1024)S(1)}, f32[2048]{0:T(1024)S(1)}, u32[]{:S(2)}, u32[]{:S(2)}) collective-permute-start(f32[2048]{0:T(1024)S(1)} %add.245), channel_id=1, source_target_pairs={{0,2},{1,3},{2,0},{3,1},{4,6},{5,7},{6,4},{7,5},{8,10},{9,11},{10,... | collective-permute-start | bytes 24584 | tf_op jit(solution)/shard_map/ppermute | solution.py:26
  23.0 4.0 %collective-permute-start.2 = (f32[2048]{0:T(1024)S(1)}, f32[2048]{0:T(1024)S(1)}, u32[]{:S(2)}, u32[]{:S(2)}) collective-permute-start(f32[2048]{0:T(1024)S(1)} %add.246), channel_id=1, source_target_pairs={{0,4},{1,5},{2,6},{3,7},{4,0},{5,1},{6,2},{7,3},{8,12},{9,13},{10,... | collective-permute-start | bytes 24584 | tf_op jit(solution)/shard_map/ppermute | solution.py:26
  27.0 33.8 %all-to-all-start = ((bf16[32,8,2048]{2,1,0:T(8,128)(2,1)}), bf16[32,8,2048]{2,1,0:T(8,128)(2,1)}, u32[]{:S(2)}, u32[]{:S(2)}) async-start(bf16[32,8,2048]{2,1,0:T(8,128)(2,1)} %bitcast.12), calls=%async_computation | async-start | bytes 2097152 | tf_op jit(solution)/shard_map/all_to_all | solution.py:109
  42.0 3.6 %copy-start.23 = (s32[64]{0:T(128)S(1)}, s32[64]{0:T(128)}, u32[]{:S(2)}) copy-start(s32[64]{0:T(128)} %multiply_add_fusion.2) | copy-start | bytes 772
  46.1 5.4 %copy-start.12 = (f32[512,64]{0,1:T(8,128)}, f32[512,64]{0,1:T(8,128)S(1)}, u32[]{:S(2)}) copy-start(f32[512,64]{0,1:T(8,128)S(1)} %get-tuple-element.52) | copy-start | bytes 393220
  46.2 5.4 %copy-start.14 = (f32[512,64]{0,1:T(8,128)}, f32[512,64]{0,1:T(8,128)S(1)}, u32[]{:S(2)}) copy-start(f32[512,64]{0,1:T(8,128)S(1)} %get-tuple-element.53) | copy-start | bytes 393220
  46.4 5.1 %copy-start.26 = (s32[2]{0:T(128)S(1)}, s32[2]{0:T(128)}, u32[]{:S(2)}) copy-start(s32[2]{0:T(128)} %iota_multiply_fusion.1) | copy-start | bytes 28
  46.4 5.3 %copy-start.19 = (f32[128,64]{0,1:T(8,128)S(1)}, f32[128,64]{0,1:T(8,128)}, u32[]{:S(2)}) copy-start(f32[128,64]{0,1:T(8,128)} %get-tuple-element.54) | copy-start | bytes 98308
  46.4 5.3 %copy-start.20 = (f32[128,64]{0,1:T(8,128)S(1)}, f32[128,64]{0,1:T(8,128)}, u32[]{:S(2)}) copy-start(f32[128,64]{0,1:T(8,128)} %get-tuple-element.55) | copy-start | bytes 98308
  46.4 5.3 %copy-start.5 = (bf16[512,512]{1,0:T(8,128)(2,1)S(1)}, bf16[512,512]{1,0:T(8,128)(2,1)}, u32[]{:S(2)}) copy-start(bf16[512,512]{1,0:T(8,128)(2,1)} %copy.109) | copy-start | bytes 1572868
  46.4 5.3 %copy-start.6 = (bf16[512,512]{1,0:T(8,128)(2,1)S(1)}, bf16[512,512]{1,0:T(8,128)(2,1)}, u32[]{:S(2)}) copy-start(bf16[512,512]{1,0:T(8,128)(2,1)} %copy.110) | copy-start | bytes 1572868
  46.5 5.3 %copy-start.7 = (bf16[512,512]{1,0:T(8,128)(2,1)S(1)}, bf16[512,512]{1,0:T(8,128)(2,1)}, u32[]{:S(2)}) copy-start(bf16[512,512]{1,0:T(8,128)(2,1)} %copy.113) | copy-start | bytes 1572868
  46.5 5.3 %copy-start.25 = (pred[2]{0:T(512)(128)(4,1)S(1)}, pred[2]{0:T(512)(128)(4,1)}, u32[]{:S(2)}) copy-start(pred[2]{0:T(512)(128)(4,1)} %iota_compare_fusion.1) | copy-start | bytes 10
  60.9 28.6 %all-to-all-start.1 = ((bf16[32,8,2048]{2,1,0:T(8,128)(2,1)}), bf16[32,8,2048]{2,1,0:T(8,128)(2,1)S(1)}, u32[]{:S(2)}, u32[]{:S(2)}) async-start(bf16[32,8,2048]{2,1,0:T(8,128)(2,1)} %bitcast.35), calls=%async_computation.1 | async-start | bytes 2097152 | tf_op jit(solution)/shard_map/all_to_all | solution.py:111
  68.1 2.2 %copy-start.3 = (f32[128,512]{1,0:T(8,128)S(1)}, f32[128,512]{1,0:T(8,128)}, u32[]{:S(2)}) copy-start(f32[128,512]{1,0:T(8,128)} %get-tuple-element.57) | copy-start | bytes 786436
  70.3 1.3 copy-start.16
  70.3 1.3 copy-start.27
  71.6 2.5 %copy-start.2 = (f32[8,128,2,512]{3,1,2,0:T(8,128)S(1)}, f32[8,128,2,512]{3,1,2,0:T(8,128)}, u32[]{:S(2)}) copy-start(f32[8,128,2,512]{3,1,2,0:T(8,128)} %fusion.40) | copy-start | bytes 12582916
  74.1 2.2 %copy-start = (f32[8,128,2,512]{3,1,2,0:T(8,128)}, f32[8,128,2,512]{3,1,2,0:T(8,128)S(1)}, u32[]{:S(2)}) copy-start(f32[8,128,2,512]{3,1,2,0:T(8,128)S(1)} %convolution_bitcast_fusion.3) | copy-start | bytes 12582916
  74.1 2.2 %copy-start.10 = (bf16[2,512,512]{2,1,0:T(8,128)(2,1)S(1)}, bf16[2,512,512]{2,1,0:T(8,128)(2,1)}, u32[]{:S(2)}) copy-start(bf16[2,512,512]{2,1,0:T(8,128)(2,1)} %get-tuple-element.46) | copy-start | bytes 3145732
  76.4 2.5 %copy-start.11 = (f32[128,512]{1,0:T(8,128)S(1)}, f32[128,512]{1,0:T(8,128)}, u32[]{:S(2)}) copy-start(f32[128,512]{1,0:T(8,128)} %fusion.50) | copy-start | bytes 786436
  89.5 30.4 %all-to-all-start.2 = ((bf16[8,32,2048]{2,0,1:T(8,128)(2,1)}), bf16[8,32,2048]{2,0,1:T(8,128)(2,1)S(1)}, u32[]{:S(2)}, u32[]{:S(2)}) async-start(bf16[8,32,2048]{2,0,1:T(8,128)(2,1)} %bitcast.47), calls=%async_computation.2 | async-start | bytes 2097152 | tf_op jit(solution)/shard_map/all_to_all | solution.py:166
  101.3 1.4 copy-start.17
  102.6 2.5 %copy-start.1 = (f32[8,128,2,512]{3,1,2,0:T(8,128)S(1)}, f32[8,128,2,512]{3,1,2,0:T(8,128)}, u32[]{:S(2)}) copy-start(f32[8,128,2,512]{3,1,2,0:T(8,128)} %copy-done) | copy-start | bytes 12582916
  106.4 1.9 %copy-start.18 = (f32[128,64]{1,0:T(8,128)S(1)}, f32[128,64]{1,0:T(8,128)}, u32[]{:S(2)}) copy-start(f32[128,64]{1,0:T(8,128)} %copy.121) | copy-start | bytes 98308
  108.3 11.6 %copy-start.21 = (f32[256]{0:T(256)S(1)}, f32[256]{0:T(256)}, u32[]{:S(2)}) copy-start(f32[256]{0:T(256)} %param.9) | copy-start | bytes 3076
  121.7 9.3 %collective-permute-start.3 = (f32[2048]{0:T(1024)S(1)}, f32[2048]{0:T(1024)S(1)}, u32[]{:S(2)}, u32[]{:S(2)}) collective-permute-start(f32[2048]{0:T(1024)S(1)} %fusion.3), channel_id=1, source_target_pairs={{0,1},{1,0},{2,3},{3,2},{4,5},{5,4},{6,7},{7,6},{8,9},{9,8},{10,11... | collective-permute-start | bytes 24584 | tf_op jit(solution)/shard_map/ppermute | solution.py:26
  131.0 14.8 %collective-permute-start.4 = (f32[2048]{0:T(1024)S(1)}, f32[2048]{0:T(1024)S(1)}, u32[]{:S(2)}, u32[]{:S(2)}) collective-permute-start(f32[2048]{0:T(1024)S(1)} %add.267), channel_id=1, source_target_pairs={{0,2},{1,3},{2,0},{3,1},{4,6},{5,7},{6,4},{7,5},{8,10},{9,11},{10,... | collective-permute-start | bytes 24584 | tf_op jit(solution)/shard_map/ppermute | solution.py:26
  145.8 4.1 %collective-permute-start.5 = (f32[2048]{0:T(1024)S(1)}, f32[2048]{0:T(1024)S(1)}, u32[]{:S(2)}, u32[]{:S(2)}) collective-permute-start(f32[2048]{0:T(1024)S(1)} %add.268), channel_id=1, source_target_pairs={{0,4},{1,5},{2,6},{3,7},{4,0},{5,1},{6,2},{7,3},{8,12},{9,13},{10,... | collective-permute-start | bytes 24584 | tf_op jit(solution)/shard_map/ppermute | solution.py:26
  (5 other events, 6.0 us)

commit v4 on v3

--- a/solution.py
+++ b/solution.py
@@ -163,9 +163,17 @@
         - partial[..., FEAT:] * block_sin[None, :, None, :],
         axis=1,
     ).transpose(2, 1, 0)
-    home_field = lax.all_to_all(time_field, "seq", split_axis=1, concat_axis=0, tiled=True)
-    coef_local, home_field = lax.optimization_barrier((coef_local, home_field))
-    coef_sum = lax.all_to_all(coef_local, "seq", split_axis=0, concat_axis=2, tiled=True)
+    coef_rows = FEAT // seq_parts
+    coef_blocks = coef_local.reshape(seq_parts, coef_rows * 2, width_share).transpose(2, 0, 1)
+    coef_high = coef_blocks.astype(jnp.bfloat16)
+    coef_low = (coef_blocks - coef_high.astype(jnp.float32)).astype(jnp.bfloat16)
+    outgoing = jnp.concatenate(
+        [time_field.reshape(width_share, seq_parts, local_tokens), coef_high, coef_low], axis=2
+    )
+    incoming = lax.all_to_all(outgoing, "seq", split_axis=1, concat_axis=0, tiled=True)
+    home_field = incoming[:, 0, :local_tokens]
+    coef_parts = incoming[:, 0, local_tokens:].astype(jnp.float32).reshape(local_width, 2, coef_rows, 2)
+    coef_sum = (coef_parts[:, 0] + coef_parts[:, 1]).transpose(1, 2, 0)
     filter_grad = coef_sum / math.sqrt(seq_total)
     conv_grad = home_field.T.astype(jnp.float32)
     normed_grad = conv_grad + skip_weight[None, :] * gated.astype(jnp.float32)

time: 156 us -> 154 us (0.987)
  blocking collectives: 13.4 us -> 35.2 us
  starting transfers between devices: 42.8 us -> 31.6 us
  waiting for transfers between devices: 31 us -> 20 us
    all_to_all x1, blocking collectives: 13.4 us -> 35.2 us  [per_device(): lax.all_to_all(outgoing, 'seq', split_axis=1, concat_axis=0, tiled=True)]
    all_to_all x1 -> x0, waiting for transfers between devices: 11.2 us -> none  [per_device(): lax.all_to_all(time_field, 'seq', split_axis=1, concat_axis=0, tiled=True)]
    all_to_all x1 -> x0, starting transfers between devices: 9.34 us -> none  [per_device(): lax.all_to_all(time_field, 'seq', split_axis=1, concat_axis=0, tiled=True)]
    all_to_all x1, waiting for transfers between devices: 6.13 us -> 3.87 us  [per_device(): lax.all_to_all(gated.T, 'seq', split_axis=0, concat_axis=1, tiled=True)]
    ppermute x6, starting transfers between devices: 16.6 us -> 14.8 us  [taken_together(): value = value + lax.ppermute(value, axis, pairs)]
    unnamed x60 -> x69, local copies, waits for them, and re-layouts: 8.88 us -> 7.62 us
  transfers between devices with their start and end apart: 9 -> 8, of which waited for: 7 -> 7; matrix products, arithmetic and copies ran while one was open for 36% -> 30% of each run, Pallas kernels for 0% -> 0%
where the time goes in v4:
time: 154 us; the launch traced here: 152 us
  blocking collectives  35.2 us (23%)
  starting transfers between devices  31.6 us (21%)
  other arithmetic  28.4 us (18%)
  waiting for transfers between devices  20 us (13%)
  local copies, waits for them, and re-layouts  18.1 us (12%)
  matrix products  17.9 us (12%)
    all_to_all x1, blocking collectives, per_device(): lax.all_to_all(outgoing, 'seq', split_axis=1, concat_axis=0, tiled=True)  35.2 us
    ppermute x6, starting transfers between devices, taken_together(): value = value + lax.ppermute(value, axis, pairs)  14.8 us
    all_to_all x1, starting transfers between devices, per_device(): lax.all_to_all(gated.T, 'seq', split_axis=0, concat_axis=1, tiled=True)  9.63 us
    all_to_all x1, waiting for transfers between devices, per_device(): lax.all_to_all(normed.T, 'seq', split_axis=0, concat_axis=1, tiled=True)  9.15 us
    unnamed x69, local copies, waits for them, and re-layouts  7.62 us
    all_to_all x1, starting transfers between devices, per_device(): lax.all_to_all(normed.T, 'seq', split_axis=0, concat_axis=1, tiled=True)  7.19 us
    ppermute x6, waiting for transfers between devices, taken_together(): value = value + lax.ppermute(value, axis, pairs)  6.99 us
    another operation x8, other arithmetic  5.78 us
  transfers between devices with their start and end apart: 8, of which 7 were waited for; matrix products, arithmetic and copies ran while one was open for 30% of the time, Pallas kernels for 0%

profile of v4, /device:TPU:1, one launch (start us, length us, event | category | flops | bytes accessed | tf_op | source)
XLA Modules:
  0.0 152.4 jit_solution(498138596995253078)
XLA Ops:
  0.6 1.5 copy.134
  2.4 3.3 %collective-permute-start = (f32[2048]{0:T(1024)S(1)}, f32[2048]{0:T(1024)S(1)}, u32[]{:S(2)}, u32[]{:S(2)}) collective-permute-start(f32[2048]{0:T(1024)S(1)} %fusion), channel_id=1, source_target_pairs={{0,1},{1,0},{2,3},{3,2},{4,5},{5,4},{6,7},{7,6},{8,9},{9,8},{10,11... | collective-permute-start | bytes 24584 | tf_op jit(solution)/shard_map/ppermute | solution.py:26
  8.8 1.6 %fusion.52 = (f32[128,512]{1,0:T(8,128)S(1)}, f32[128,512]{1,0:T(8,128)}) fusion(), kind=kLoop, calls=%fused_computation.84 | loop fusion | flops 262144 | bytes 524288 | tf_op jit(solution)/shard_map/cos | solution.py:58
  10.5 1.6 %fusion.51 = f32[128,512]{1,0:T(8,128)} fusion(), kind=kLoop, calls=%fused_computation.83 | loop fusion | flops 196608 | bytes 262144 | tf_op jit(solution)/shard_map/sin | solution.py:59
  12.0 2.3 %copy.133 = bf16[2048,256]{0,1:T(8,128)(2,1)} copy(bf16[2048,256]{1,0:T(8,128)(2,1)} %param.7) | data formatting | bytes 2097152 | tf_op args[1]
  15.6 2.3 %broadcast_select_fusion.2 = bf16[2048,256]{0,1:T(8,128)(2,1)} fusion(bf16[2048,256]{0,1:T(8,128)(2,1)} %copy.133, pred[2048]{0:T(1024)(128)(4,1)S(1)} %fusion.98), kind=kLoop, calls=%fused_computation.77 | loop fusion | flops 524288 | bytes 2099200 | tf_op jit(solution)/shard_map/jit(_where)/select_n | solution.py:99
  19.9 1.9 %collective-permute-done.1 = f32[2048]{0:T(1024)S(1)} collective-permute-done((f32[2048]{0:T(1024)S(1)}, f32[2048]{0:T(1024)S(1)}, u32[]{:S(2)}, u32[]{:S(2)}) %collective-permute-start.1) | collective-permute-done | bytes 8224 | tf_op jit(solution)/shard_map/ppermute | solution.py:26
  23.4 2.4 %collective-permute-done.2 = f32[2048]{0:T(1024)S(1)} collective-permute-done((f32[2048]{0:T(1024)S(1)}, f32[2048]{0:T(1024)S(1)}, u32[]{:S(2)}, u32[]{:S(2)}) %collective-permute-start.2) | collective-permute-done | bytes 8224 | tf_op jit(solution)/shard_map/ppermute | solution.py:26
  25.8 9.6 %all-to-all-start = ((bf16[32,8,2048]{2,1,0:T(8,128)(2,1)}), bf16[32,8,2048]{2,1,0:T(8,128)(2,1)}, u32[]{:S(2)}, u32[]{:S(2)}) async-start(bf16[32,8,2048]{2,1,0:T(8,128)(2,1)} %bitcast.11), calls=%async_computation | async-start | bytes 2097152 | tf_op jit(solution)/shard_map/all_to_all | solution.py:109
  37.7 2.0 %copy.145 = bf16[512,512]{1,0:T(8,128)(2,1)} copy(bf16[512,512]{0,1:T(8,128)(2,1)} %get-tuple-element.58) | data formatting | bytes 1048576 | tf_op jit(solution)/shard_map/neg | solution.py:51
  40.7 2.1 %copy.142 = bf16[512,512]{1,0:T(8,128)(2,1)} copy(bf16[512,512]{0,1:T(8,128)(2,1)} %get-tuple-element.59) | data formatting | bytes 1048576 | tf_op jit(solution)/shard_map/neg | solution.py:51
  44.1 1.5 copy.153
  45.6 1.2 fusion.72
  47.2 5.1 %fusion.41 = f32[8,128,2,512]{3,1,2,0:T(8,128)} fusion(f32[8,128,2,64]{3,1,2,0:T(8,128)S(1)} %get-tuple-element.42, f32[8,128,2,64]{3,1,2,0:T(8,128)S(1)} %get-tuple-element.41, f32[512,64]{0,1:T(8,128)S(1)} %get-tuple-element.53, f32[512,64]{0,1:T(8,128)S(1)} %get-tuple-element.52), kind=kOutput, calls=%fused_computation.63 | convolution fusion | flops 1610940416 | bytes 5505024 | tf_op jit(solution)/shard_map/ckrj,bj->ckrb/dot_general | solution.py:131
  53.0 1.4 broadcast_select_fusion
  54.5 1.3 fusion.2
  55.8 3.9 %all-to-all-done = bf16[32,8,2048]{2,1,0:T(8,128)(2,1)} async-done(((bf16[32,8,2048]{2,1,0:T(8,128)(2,1)}), bf16[32,8,2048]{2,1,0:T(8,128)(2,1)}, u32[]{:S(2)}, u32[]{:S(2)}) %all-to-all-start) | async-done | bytes 1048608 | tf_op jit(solution)/shard_map/all_to_all | solution.py:109
  59.6 7.2 %all-to-all-start.1 = ((bf16[32,8,2048]{2,1,0:T(8,128)(2,1)}), bf16[32,8,2048]{2,1,0:T(8,128)(2,1)S(1)}, u32[]{:S(2)}, u32[]{:S(2)}) async-start(bf16[32,8,2048]{2,1,0:T(8,128)(2,1)} %bitcast.34), calls=%async_computation.1 | async-start | bytes 2097152 | tf_op jit(solution)/shard_map/all_to_all | solution.py:111
  66.9 2.2 %convolution_bitcast_fusion.4 = f32[8,128,2,512]{3,1,0,2:T(8,128)S(1)} fusion(bf16[8,128,512]{2,0,1:T(8,128)(2,1)} %bitcast.14, bf16[128,128,1]{0,1,2:T(8,128)(2,1)S(1)} %bitcast.140, bf16[128,128,1]{0,1,2:T(8,128)(2,1)S(1)} %bitcast.142), kind=kOutput, calls=%fused_computation.10 | convolution fusion | flops 268566528 | bytes 5308416 | tf_op jit(solution)/shard_map/cnm,nkr->ckrm/dot_general | solution.py:117
  70.1 2.5 %convolution_bitcast_fusion.3 = f32[8,128,2,512]{3,1,2,0:T(8,128)S(1)} fusion(bf16[2,512,512]{2,1,0:T(8,128)(2,1)S(1)} %get-tuple-element.47, bf16[512,512]{1,0:T(8,128)(2,1)S(1)} %copy-done.17, pred[2,2]{0,1:T(4,128)(4,1)S(1)} %copy-done.31, bf16[8,128,1,512]{3,1,0,2:T(8,128)(2,1)S(1)} %get-tuple-element.35, bf16[8,128,1,512]{3,1,0,2:T(8,128)(2,1)S(1)} %get-tuple-element.34), kind=kOutput, calls=%fused_computation.9 | convolution fusion | flops 2149580800 | bytes 7864324 | tf_op jit(solution)/shard_map/ckrm,rmsj->cksj/dot_general | solution.py:121
  72.6 1.3 add_convert_fusion.3
  74.8 2.5 %convolution_bitcast_fusion.2 = f32[8,128,2,512]{3,1,0,2:T(8,128)S(1)} fusion(bf16[8,128,1,512]{3,1,2,0:T(8,128)(2,1)S(1)} %get-tuple-element.29, bf16[8,128,1,512]{3,1,2,0:T(8,128)(2,1)S(1)} %get-tuple-element.28, bf16[2,512,512]{2,1,0:T(8,128)(2,1)S(1)} %copy-done.11, bf16[512,512]{1,0:T(8,128)(2,1)S(1)} %copy-done.17, pred[2,2]{0,1:T(4,128)(4,1)S(1)} %copy-done.31), kind=kOutput, calls=%fused_computation.8 | convolution fusion | flops 2152726528 | bytes 7864324 | tf_op jit(solution)/shard_map/ckrm,rmsj->cksj/dot_general | solution.py:138
  79.1 9.1 %all-to-all-done.1 = bf16[32,8,2048]{2,1,0:T(8,128)(2,1)S(1)} async-done(((bf16[32,8,2048]{2,1,0:T(8,128)(2,1)}), bf16[32,8,2048]{2,1,0:T(8,128)(2,1)S(1)}, u32[]{:S(2)}, u32[]{:S(2)}) %all-to-all-start.1) | async-done | bytes 1048608 | tf_op jit(solution)/shard_map/all_to_all | solution.py:111
  90.6 2.5 %convolution_bitcast_fusion = f32[8,128,2,512]{3,1,2,0:T(8,128)S(1)} fusion(bf16[2,512,512]{2,1,0:T(8,128)(2,1)S(1)} %copy-done.10, bf16[512,512]{1,0:T(8,128)(2,1)S(1)} %copy-done.18, pred[2,2]{0,1:T(4,128)(4,1)S(1)} %copy-done.31, bf16[8,128,1,512]{3,1,0,2:T(8,128)(2,1)S(1)} %get-tuple-element.31, bf16[8,128,1,512]{3,1,0,2:T(8,128)(2,1)S(1)} %get-tuple-element.30), kind=kOutput, calls=%fused_computation.6 | convolution fusion | flops 2149580800 | bytes 7864324 | tf_op jit(solution)/shard_map/ckrm,rmsj->cksj/dot_general | solution.py:121
  93.1 1.5 add_convert_fusion
  94.6 1.8 %fusion.17 = f32[8,128,2,128]{3,1,2,0:T(8,128)S(1)} fusion(bf16[8,128,1,512]{3,1,2,0:T(8,128)(2,1)S(1)} %get-tuple-element.27, bf16[8,128,1,512]{3,1,2,0:T(8,128)(2,1)S(1)} %get-tuple-element.26, f32[512,64]{0,1:T(8,128)S(1)} %copy-done.16, f32[512,64]{0,1:T(8,128)S(1)} %copy-done.14), kind=kOutput, calls=%fused_computation.29 | convolution fusion | flops 1611726848 | bytes 3407872 | tf_op jit(solution)/shard_map/ckrb,bj->ckrj/dot_general | solution.py:157
  98.3 35.2 %all_to_all.56 = bf16[8,32,2056]{2,0,1:T(8,128)(2,1)S(1)} all-to-all(bf16[8,32,2056]{2,0,1:T(8,128)(2,1)S(1)} %concatenate.11), channel_id=1, replica_groups=mesh['seq'=32,'ch'=8] {'seq'}, dimensions={1} | all-to-all | bytes 2105344 | tf_op jit(solution)/shard_map/all_to_all | solution.py:173
  133.5 1.8 %fusion.3 = f32[2048]{0:T(1024)S(1)} fusion(bf16[2048,256]{0,1:T(8,128)(2,1)S(1)} %copy.134, bf16[2048,256]{0,1:T(8,128)(2,1)} %broadcast_select_fusion.2, f32[256]{0:T(256)S(1)} %copy-done.25, f32[256]{0:T(256)S(1)} %copy-done.24, bf16[256,1,2056]{2,0,1:T(8,128)(2,1)S(1)} %bitcast.132), kind=kLoop, calls=%fused_computation.14 | loop fusion | flops 4192256 | bytes 3155968 | tf_op jit(solution)/shard_map/reduce_sum | solution.py:181
  135.4 6.4 %collective-permute-start.3 = (f32[2048]{0:T(1024)S(1)}, f32[2048]{0:T(1024)S(1)}, u32[]{:S(2)}, u32[]{:S(2)}) collective-permute-start(f32[2048]{0:T(1024)S(1)} %fusion.3), channel_id=1, source_target_pairs={{0,1},{1,0},{2,3},{3,2},{4,5},{5,4},{6,7},{7,6},{8,9},{9,8},{10,11... | collective-permute-start | bytes 24584 | tf_op jit(solution)/shard_map/ppermute | solution.py:26
  145.1 2.7 %collective-permute-start.5 = (f32[2048]{0:T(1024)S(1)}, f32[2048]{0:T(1024)S(1)}, u32[]{:S(2)}, u32[]{:S(2)}) collective-permute-start(f32[2048]{0:T(1024)S(1)} %add.272), channel_id=1, source_target_pairs={{0,4},{1,5},{2,6},{3,7},{4,0},{5,1},{6,2},{7,3},{8,12},{9,13},{10,... | collective-permute-start | bytes 24584 | tf_op jit(solution)/shard_map/ppermute | solution.py:26
  149.1 1.9 %fusion.5 = bf16[2048,256]{0,1:T(8,128)(2,1)S(1)} fusion(bf16[2048,256]{0,1:T(8,128)(2,1)S(1)} %copy.134, bf16[2048,256]{0,1:T(8,128)(2,1)} %broadcast_select_fusion.2, f32[2048]{0:T(1024)S(1)} %fusion.100, f32[256]{0:T(256)S(1)} %copy-done.25, f32[256]{0:T(256)S(1)} %copy-done.24, f32[2048]{0:T(1024)S(1)} %add_rsqrt_fusion, ...), kind=kLoop, calls=%fused_computation.16 | loop fusion | flops 5242880 | bytes 4212736 | tf_op jit(solution)/shard_map/convert_element_type | solution.py:185
  151.1 1.3 copy.159
  (125 shorter events, 26.1 us)
Async XLA Ops:
  2.4 16.9 %collective-permute-start = (f32[2048]{0:T(1024)S(1)}, f32[2048]{0:T(1024)S(1)}, u32[]{:S(2)}, u32[]{:S(2)}) collective-permute-start(f32[2048]{0:T(1024)S(1)} %fusion), channel_id=1, source_target_pairs={{0,1},{1,0},{2,3},{3,2},{4,5},{5,4},{6,7},{7,6},{8,9},{9,8},{10,11... | collective-permute-start | bytes 24584 | tf_op jit(solution)/shard_map/ppermute | solution.py:26
  5.6 9.1 %copy-start.26 = (s32[64]{0:T(128)}, s32[64]{0:T(128)S(1)}, u32[]{:S(2)}) copy-start(s32[64]{0:T(128)S(1)} %multiply_add_fusion.2) | copy-start | bytes 772
  7.1 7.2 %copy-start.27 = (s32[64]{0:T(128)S(1)}, s32[64]{0:T(128)}, u32[]{:S(2)}) copy-start(s32[64]{0:T(128)} %param.11) | copy-start | bytes 772
  17.9 18.2 %copy-start.30 = (bf16[256]{0:T(256)(128)(2,1)S(1)}, bf16[256]{0:T(256)(128)(2,1)}, u32[]{:S(2)}) copy-start(bf16[256]{0:T(256)(128)(2,1)} %param.8) | copy-start | bytes 1540
  19.2 2.6 %collective-permute-start.1 = (f32[2048]{0:T(1024)S(1)}, f32[2048]{0:T(1024)S(1)}, u32[]{:S(2)}, u32[]{:S(2)}) collective-permute-start(f32[2048]{0:T(1024)S(1)} %add.249), channel_id=1, source_target_pairs={{0,2},{1,3},{2,0},{3,1},{4,6},{5,7},{6,4},{7,5},{8,10},{9,11},{10,... | collective-permute-start | bytes 24584 | tf_op jit(solution)/shard_map/ppermute | solution.py:26
  21.8 4.0 %collective-permute-start.2 = (f32[2048]{0:T(1024)S(1)}, f32[2048]{0:T(1024)S(1)}, u32[]{:S(2)}, u32[]{:S(2)}) collective-permute-start(f32[2048]{0:T(1024)S(1)} %add.250), channel_id=1, source_target_pairs={{0,4},{1,5},{2,6},{3,7},{4,0},{5,1},{6,2},{7,3},{8,12},{9,13},{10,... | collective-permute-start | bytes 24584 | tf_op jit(solution)/shard_map/ppermute | solution.py:26
  25.8 33.8 %all-to-all-start = ((bf16[32,8,2048]{2,1,0:T(8,128)(2,1)}), bf16[32,8,2048]{2,1,0:T(8,128)(2,1)}, u32[]{:S(2)}, u32[]{:S(2)}) async-start(bf16[32,8,2048]{2,1,0:T(8,128)(2,1)} %bitcast.11), calls=%async_computation | async-start | bytes 2097152 | tf_op jit(solution)/shard_map/all_to_all | solution.py:109
  40.7 2.3 %copy-start.8 = (bf16[512,8,64]{0,2,1:T(8,128)(2,1)S(1)}, bf16[512,8,64]{0,2,1:T(8,128)(2,1)}, u32[]{:S(2)}) copy-start(bf16[512,8,64]{0,2,1:T(8,128)(2,1)} %subtract_multiply_fusion) | copy-start | bytes 1572868
  46.8 5.4 %copy-start.13 = (f32[512,64]{0,1:T(8,128)}, f32[512,64]{0,1:T(8,128)S(1)}, u32[]{:S(2)}) copy-start(f32[512,64]{0,1:T(8,128)S(1)} %get-tuple-element.52) | copy-start | bytes 393220
  46.8 5.4 %copy-start.15 = (f32[512,64]{0,1:T(8,128)}, f32[512,64]{0,1:T(8,128)S(1)}, u32[]{:S(2)}) copy-start(f32[512,64]{0,1:T(8,128)S(1)} %get-tuple-element.53) | copy-start | bytes 393220
  47.1 5.1 %copy-start.29 = (s32[2]{0:T(128)S(1)}, s32[2]{0:T(128)}, u32[]{:S(2)}) copy-start(s32[2]{0:T(128)} %iota_multiply_fusion.1) | copy-start | bytes 28
  47.1 5.3 %copy-start.20 = (f32[128,64]{0,1:T(8,128)S(1)}, f32[128,64]{0,1:T(8,128)}, u32[]{:S(2)}) copy-start(f32[128,64]{0,1:T(8,128)} %get-tuple-element.54) | copy-start | bytes 98308
  47.1 5.3 %copy-start.21 = (f32[128,64]{0,1:T(8,128)S(1)}, f32[128,64]{0,1:T(8,128)}, u32[]{:S(2)}) copy-start(f32[128,64]{0,1:T(8,128)} %get-tuple-element.55) | copy-start | bytes 98308
  47.1 5.9 %copy-start.5 = (bf16[512,512]{1,0:T(8,128)(2,1)S(1)}, bf16[512,512]{1,0:T(8,128)(2,1)}, u32[]{:S(2)}) copy-start(bf16[512,512]{1,0:T(8,128)(2,1)} %copy.144) | copy-start | bytes 1572868
  47.1 5.9 %copy-start.6 = (bf16[512,512]{1,0:T(8,128)(2,1)S(1)}, bf16[512,512]{1,0:T(8,128)(2,1)}, u32[]{:S(2)}) copy-start(bf16[512,512]{1,0:T(8,128)(2,1)} %copy.145) | copy-start | bytes 1572868
  47.1 5.9 %copy-start.7 = (bf16[512,512]{1,0:T(8,128)(2,1)S(1)}, bf16[512,512]{1,0:T(8,128)(2,1)}, u32[]{:S(2)}) copy-start(bf16[512,512]{1,0:T(8,128)(2,1)} %copy.142) | copy-start | bytes 1572868
  47.1 5.9 %copy-start.28 = (pred[2]{0:T(512)(128)(4,1)S(1)}, pred[2]{0:T(512)(128)(4,1)}, u32[]{:S(2)}) copy-start(pred[2]{0:T(512)(128)(4,1)} %iota_compare_fusion.1) | copy-start | bytes 10
  54.5 15.4 %copy-start.9 = (bf16[2,512,512]{2,1,0:T(8,128)(2,1)}, bf16[2,512,512]{2,1,0:T(8,128)(2,1)S(1)}, u32[]{:S(2)}) copy-start(bf16[2,512,512]{2,1,0:T(8,128)(2,1)S(1)} %get-tuple-element.47) | copy-start | bytes 3145732
  59.6 28.6 %all-to-all-start.1 = ((bf16[32,8,2048]{2,1,0:T(8,128)(2,1)}), bf16[32,8,2048]{2,1,0:T(8,128)(2,1)S(1)}, u32[]{:S(2)}, u32[]{:S(2)}) async-start(bf16[32,8,2048]{2,1,0:T(8,128)(2,1)} %bitcast.34), calls=%async_computation.1 | async-start | bytes 2097152 | tf_op jit(solution)/shard_map/all_to_all | solution.py:111
  66.8 2.2 %copy-start.3 = (f32[128,512]{1,0:T(8,128)S(1)}, f32[128,512]{1,0:T(8,128)}, u32[]{:S(2)}) copy-start(f32[128,512]{1,0:T(8,128)} %get-tuple-element.57) | copy-start | bytes 786436
  70.1 2.5 %copy-start.2 = (f32[8,128,2,512]{3,1,2,0:T(8,128)S(1)}, f32[8,128,2,512]{3,1,2,0:T(8,128)}, u32[]{:S(2)}) copy-start(f32[8,128,2,512]{3,1,2,0:T(8,128)} %fusion.41) | copy-start | bytes 12582916
  72.6 2.2 %copy-start = (f32[8,128,2,512]{3,1,2,0:T(8,128)}, f32[8,128,2,512]{3,1,2,0:T(8,128)S(1)}, u32[]{:S(2)}) copy-start(f32[8,128,2,512]{3,1,2,0:T(8,128)S(1)} %convolution_bitcast_fusion.3) | copy-start | bytes 12582916
  72.6 2.2 %copy-start.11 = (bf16[2,512,512]{2,1,0:T(8,128)(2,1)S(1)}, bf16[2,512,512]{2,1,0:T(8,128)(2,1)}, u32[]{:S(2)}) copy-start(bf16[2,512,512]{2,1,0:T(8,128)(2,1)} %get-tuple-element.46) | copy-start | bytes 3145732
  74.8 2.5 %copy-start.12 = (f32[128,512]{1,0:T(8,128)S(1)}, f32[128,512]{1,0:T(8,128)}, u32[]{:S(2)}) copy-start(f32[128,512]{1,0:T(8,128)} %fusion.51) | copy-start | bytes 786436
  90.6 2.5 %copy-start.1 = (f32[8,128,2,512]{3,1,2,0:T(8,128)S(1)}, f32[8,128,2,512]{3,1,2,0:T(8,128)}, u32[]{:S(2)}) copy-start(f32[8,128,2,512]{3,1,2,0:T(8,128)} %copy-done) | copy-start | bytes 12582916
  93.1 1.5 copy-start.14
  93.1 1.5 copy-start.16
  94.6 1.9 %copy-start.19 = (f32[128,64]{1,0:T(8,128)S(1)}, f32[128,64]{1,0:T(8,128)}, u32[]{:S(2)}) copy-start(f32[128,64]{1,0:T(8,128)} %copy.153) | copy-start | bytes 98308
  97.4 36.2 %copy-start.25 = (f32[256]{0:T(256)S(1)}, f32[256]{0:T(256)}, u32[]{:S(2)}) copy-start(f32[256]{0:T(256)} %param.9) | copy-start | bytes 3076
  135.4 7.2 %collective-permute-start.3 = (f32[2048]{0:T(1024)S(1)}, f32[2048]{0:T(1024)S(1)}, u32[]{:S(2)}, u32[]{:S(2)}) collective-permute-start(f32[2048]{0:T(1024)S(1)} %fusion.3), channel_id=1, source_target_pairs={{0,1},{1,0},{2,3},{3,2},{4,5},{5,4},{6,7},{7,6},{8,9},{9,8},{10,11... | collective-permute-start | bytes 24584 | tf_op jit(solution)/shard_map/ppermute | solution.py:26
  142.6 2.5 %collective-permute-start.4 = (f32[2048]{0:T(1024)S(1)}, f32[2048]{0:T(1024)S(1)}, u32[]{:S(2)}, u32[]{:S(2)}) collective-permute-start(f32[2048]{0:T(1024)S(1)} %add.271), channel_id=1, source_target_pairs={{0,2},{1,3},{2,0},{3,1},{4,6},{5,7},{6,4},{7,5},{8,10},{9,11},{10,... | collective-permute-start | bytes 24584 | tf_op jit(solution)/shard_map/ppermute | solution.py:26
  145.1 4.0 %collective-permute-start.5 = (f32[2048]{0:T(1024)S(1)}, f32[2048]{0:T(1024)S(1)}, u32[]{:S(2)}, u32[]{:S(2)}) collective-permute-start(f32[2048]{0:T(1024)S(1)} %add.272), channel_id=1, source_target_pairs={{0,4},{1,5},{2,6},{3,7},{4,0},{5,1},{6,2},{7,3},{8,12},{9,13},{10,... | collective-permute-start | bytes 24584 | tf_op jit(solution)/shard_map/ppermute | solution.py:26
  (8 other events, 9.0 us)
